TPU v7x, 1024 devices: a whole 8x8x8 slice. The times are simulated.
1024 devices in a mesh: blk: 16 (over x, core), rep: 64 (over z, y).
Axes of the slice: x: 8, y: 8, z: 8, core: 2. Of those that a mesh axis runs over, the one named last changes fastest.
Arguments:
- features: bfloat16 [2048, 128, 256], P(('blk', 'rep')), may hold values from -6 to 6
- weight: bfloat16 [256, 256], replicated, may hold values from -0.375 to 0.375
- tile_values: bfloat16 [2048, 24, 128, 128], P(('blk', 'rep')), may hold values from -0.1875 to 0.1875
- tile_count: int32 [2048], P(('blk', 'rep')), may hold values from 1 to 24, as said below
- tile_cols: int32 [2048, 24], P(('blk', 'rep')), may hold values from 0 to 2047, as said below
- out_grad: bfloat16 [2048, 128, 256], P(('blk', 'rep')), may hold values from -6 to 6
- relu_mask: int32 [2048, 128, 256], P(('blk', 'rep')), may hold values 0 or 1
Outputs:
- activated: bfloat16 [2048, 128, 256], P(('blk', 'rep'))
- weight_grad: float32 [256, 256], replicated
- in_grad: bfloat16 [2048, 128, 256], P(('blk', 'rep'))
Inputs may be any that keep to these rules, and one draw needn't show every extreme that they name: `tile_count`: all 2 tile rows of some aligned block of 2 tile rows hold 24 tiles; some tile row holds one. `tile_cols`: tile rows form 64 communities: tile row t belongs to community t // 2 % 64, and every column tile of a tile row lies in its own community; the 24 column tiles of one tile row are distinct; slots not in use hold column tiles too.
All inputs are finite; a program needn't handle non-finite values. No bound on the sum of `relu_mask` on one device may be relied on, other than what follows from the above.
Results may differ from a plain program's by a relative error of at most 0.0049.
Values may be sent and summed in bfloat16 or wider, within the bound.
No kernel may reach another device: no remote copies, remote signals or barrier semaphores. Data moves between devices by JAX's collectives and lax.ppermute only.
A program may use at most 32 MiB of HBM per device.

v0:
```python
import math

import jax
import jax.numpy as jnp
from jax import lax
from jax.sharding import PartitionSpec as P


def per_device(features, weight, tile_values, tile_count, tile_cols, out_grad, relu_mask):
    row_tiles = tile_values.shape[0]
    slot_count = tile_values.shape[1]
    tile_size = tile_values.shape[2]
    feature_width = features.shape[2]
    blk_size = lax.axis_size("blk")
    rep_size = lax.axis_size("rep")
    community = blk_size * row_tiles
    local_cols = tile_cols // (rep_size * row_tiles) * row_tiles + tile_cols % row_tiles
    in_use = lax.broadcasted_iota(jnp.int32, (row_tiles, slot_count), 1) < tile_count[:, None]
    member_ids = lax.broadcasted_iota(jnp.int32, (row_tiles, slot_count, community), 2)
    one_hot = ((local_cols[:, :, None] == member_ids) & in_use[:, :, None]).astype(jnp.bfloat16)
    selected = jnp.einsum(
        "tsc,tsji->tcji", one_hot, tile_values, preferred_element_type=jnp.float32
    ).astype(jnp.bfloat16)
    gathered = lax.all_gather(features, "blk", axis=0, tiled=True)
    picked = gathered[local_cols]
    picked = jnp.where(in_use[:, :, None, None], picked, jnp.zeros((), jnp.bfloat16))
    partial_value = jnp.einsum(
        "tsji,tsjf->tif", tile_values, picked, preferred_element_type=jnp.float32
    )
    hidden = partial_value.astype(jnp.bfloat16)
    hidden_flat = hidden.reshape(-1, feature_width)
    linear = jnp.dot(hidden_flat, weight, preferred_element_type=jnp.float32)
    activated = jnp.maximum(linear, 0.0).astype(jnp.bfloat16).reshape(hidden.shape)
    grad_flat = out_grad.reshape(-1, feature_width)
    grad_term = lax.dot_general(
        hidden_flat, grad_flat, (((0,), (0,)), ((), ())), preferred_element_type=jnp.float32
    )
    node_count = row_tiles * blk_size * rep_size * tile_size
    weight_grad = lax.psum(grad_term, ("blk", "rep")) * (1.0 / math.sqrt(node_count))
    row_grad = lax.dot_general(
        grad_flat, weight, (((1,), (1,)), ((), ())), preferred_element_type=jnp.float32
    )
    row_grad = row_grad.astype(jnp.bfloat16).reshape(out_grad.shape)
    spread = lax.psum_scatter(
        jnp.einsum("tcji,tif->cjf", selected, row_grad, preferred_element_type=jnp.float32),
        "blk",
        scatter_dimension=0,
        tiled=True,
    )
    in_grad = (relu_mask.astype(jnp.float32) * spread).astype(jnp.bfloat16)
    return (activated, weight_grad, in_grad)


def solution(mesh):
    placed = (
        P(("blk", "rep"), None, None),
        P(),
        P(("blk", "rep"), None, None, None),
        P(("blk", "rep")),
        P(("blk", "rep"), None),
        P(("blk", "rep"), None, None),
        P(("blk", "rep"), None, None),
    )
    return jax.shard_map(
        per_device,
        mesh=mesh,
        in_specs=placed,
        out_specs=(P(("blk", "rep"), None, None), P(), P(("blk", "rep"), None, None)),
        check_vma=False,
    )
```

profile of v0, /device:TPU:15, one launch (start us, length us, event | category | flops | bytes accessed | tf_op | source)
XLA Modules:
  0.0 430.5 jit_solution(452583580651808914)
XLA Ops:
  7.2 0.0 copy-start
  7.2 0.0 all-gather.2.cloned.1.call-start
  7.2 0.7 all-gather.2.cloned.1.call-update
  7.9 0.0 all-reduce.2.cloned.1.call-start
  8.0 0.7 compare_select_fusion
  8.7 0.1 reshape.61
  8.7 0.7 iota_compare_fusion.1
  9.5 1.2 convolution_convert_fusion
  10.7 2.7 fusion.3
  13.4 53.7 %all-gather.2.cloned.1.call-done = bf16[32,128,256]{2,1,0:T(8,128)(2,1)} async-done(((bf16[2,128,256]{2,1,0:T(8,128)(2,1)}), bf16[32,128,256]{2,1,0:T(8,128)(2,1)}) %all-gather.2.cloned.1.call-update) | async-done | bytes 2097168 | tf_op jit(solution)/shard_map/all_gather | solution.py:24
  67.1 4.1 gather_fusion
  71.2 2.8 fusion.10
  74.0 0.0 copy-done.2
  74.0 0.9 convolution_bitcast_fusion.1
  74.9 0.0 all-reduce.2.cloned.1.call-update
  75.0 0.0 reduce-scatter.2.cloned.1.call-start
  75.0 5.0 %convolution_bitcast_fusion = f32[32,128,256]{2,1,0:T(8,128)} fusion(bf16[2,128,256,1]{2,1,0,3:T(8,128)(2,1)S(1)} %bitcast.34, bf16[2,32,128,128]{3,1,2,0:T(8,128)(2,1)} %fusion.3), kind=kOutput, calls=%fused_computation.5 | convolution fusion | flops 536870912 | bytes 6422528 | tf_op jit(solution)/shard_map/tcji,tif->cjf/dot_general | solution.py:45
  80.0 0.0 reduce-scatter.2.cloned.1.call-update
  80.0 0.9 copy-done.1
  80.9 0.8 fusion.9
  81.8 275.0 %all-reduce.2.cloned.1.call-done = f32[256,256]{1,0:T(8,128)} async-done(((f32[256,256]{1,0:T(8,128)}), f32[256,256]{1,0:T(8,128)}) %all-reduce.2.cloned.1.call-update) | async-done | bytes 262160 | tf_op jit(solution)/shard_map/psum | solution.py:39
  356.8 1.7 broadcast_multiply_fusion
  358.5 63.9 %reduce-scatter.2.cloned.1.call-done = f32[2,128,256]{2,1,0:T(8,128)} async-done(((f32[32,128,256]{2,1,0:T(8,128)}), f32[2,128,256]{2,1,0:T(8,128)}) %reduce-scatter.2.cloned.1.call-update) | async-done | bytes 262160 | tf_op jit(solution)/shard_map/reduce_scatter | solution.py:44
  422.4 1.6 multiply_convert_fusion
  (6 shorter events, 0.0 us)
Async XLA Ops:
  7.2 3.5 copy-start
  7.2 59.9 %all-gather.2.cloned.1.call-start = ((), (), s32[]{:S(2)}) async-start(), calls=%async_computation.1 | async-start | bytes 2228224 | tf_op jit(solution)/shard_map/all_gather | solution.py:24
  7.9 348.9 %all-reduce.2.cloned.1.call-start = ((), (), s32[]{:S(2)}) async-start(), calls=%async_computation.2 | async-start | bytes 524288 | tf_op jit(solution)/shard_map/psum | solution.py:39
  71.2 2.8 copy-start.2
  75.0 347.4 %reduce-scatter.2.cloned.1.call-start = ((), (), s32[]{:S(2)}) async-start(), calls=%async_computation.3 | async-start | bytes 4456448 | tf_op jit(solution)/shard_map/reduce_scatter | solution.py:44
  80.0 0.9 copy-start.1
  80.0 342.4 %copy-start.3 = (s32[2,128,256]{2,1,0:T(8,128)S(1)}, s32[2,128,256]{2,1,0:T(8,128)}, u32[]{:S(2)}) copy-start(s32[2,128,256]{2,1,0:T(8,128)} %param.13) | copy-start | bytes 786436
Sparse Core Ops, SparseCore 0:
  10.7 56.3 all-gather.1
  75.1 281.6 all-reduce.1
  360.6 61.6 reduce-scatter.1
where the time goes:
time: 431 us
  waiting for transfers between devices  393 us (91%)
  between operations  13.8 us (3%)
  matrix products  13.5 us (3%)
  local copies, waits for them, and re-layouts  5.09 us (1%)
  other arithmetic  4.73 us (1%)
    psum x1, waiting for transfers between devices, per_device(): lax.psum(grad_term, ('blk', 'rep')) * (1.0 / math.sqrt(node_count))  275 us
    reduce_scatter x1, waiting for transfers between devices, per_device(): lax.psum_scatter(jnp.einsum('tcji,tif->cjf', selected, row_grad, preferre...  63.9 us
    all_gather x1, waiting for transfers between devices, per_device(): gathered = lax.all_gather(features, 'blk', axis=0, tiled=True)  53.7 us
  transfers between devices with their start and end apart: 3, of which 3 were waited for; matrix products, arithmetic and copies ran while one was open for 3% of the time, Pallas kernels for 0%

commit v1 on v0

--- a/solution.py
+++ b/solution.py
@@ -36,7 +36,7 @@
         hidden_flat, grad_flat, (((0,), (0,)), ((), ())), preferred_element_type=jnp.float32
     )
     node_count = row_tiles * blk_size * rep_size * tile_size
-    weight_grad = lax.psum(grad_term, ("blk", "rep")) * (1.0 / math.sqrt(node_count))
+    weight_grad = _allreduce_doubling(grad_term, blk_size, rep_size) * (1.0 / math.sqrt(node_count))
     row_grad = lax.dot_general(
         grad_flat, weight, (((1,), (1,)), ((), ())), preferred_element_type=jnp.float32
     )
@@ -49,6 +49,38 @@
     )
     in_grad = (relu_mask.astype(jnp.float32) * spread).astype(jnp.bfloat16)
     return (activated, weight_grad, in_grad)
+
+
+def _bits_order(blk_size, rep_size):
+    rep_bits = [1 << b for b in range(rep_size.bit_length() - 1)]
+    blk_bits = [rep_size << b for b in range(blk_size.bit_length() - 1)]
+    return blk_bits[:1] + rep_bits + blk_bits[1:]
+
+
+def _allreduce_doubling(x, blk_size, rep_size):
+    total = blk_size * rep_size
+    for mask in _bits_order(blk_size, rep_size):
+        x = x + lax.ppermute(x, ("blk", "rep"), [(i, i ^ mask) for i in range(total)])
+    return x
+
+
+def _allreduce_halving(x, blk_size, rep_size):
+    total = blk_size * rep_size
+    me = lax.axis_index(("blk", "rep"))
+    masks = _bits_order(blk_size, rep_size)
+    flat = x.reshape(-1)
+    for mask in masks:
+        half = flat.shape[0] // 2
+        upper = (me & mask) != 0
+        lo, hi = flat[:half], flat[half:]
+        keep = jnp.where(upper, hi, lo)
+        send = jnp.where(upper, lo, hi)
+        flat = keep + lax.ppermute(send, ("blk", "rep"), [(i, i ^ mask) for i in range(total)])
+    for mask in reversed(masks):
+        upper = (me & mask) != 0
+        other = lax.ppermute(flat, ("blk", "rep"), [(i, i ^ mask) for i in range(total)])
+        flat = jnp.concatenate([jnp.where(upper, other, flat), jnp.where(upper, flat, other)])
+    return flat.reshape(x.shape)
 
 
 def solution(mesh):

time: 431 us -> 217 us (0.50)
  waiting for transfers between devices: 393 us -> 156 us
  starting transfers between devices: 0.12 us -> 24.7 us
    psum x1 -> x0, waiting for transfers between devices: 275 us -> none  [per_device(): lax.psum(grad_term, ('blk', 'rep')) * (1.0 / math.sqrt(node_count))]
    ppermute x0 -> x10, waiting for transfers between devices: none -> 104 us  [_allreduce_doubling(): lax.ppermute(x, ('blk', 'rep'), [(i, i ^ mask) for i in range(total)])]
    reduce_scatter x1, waiting for transfers between devices: 63.9 us -> 0.01 us  [per_device(): lax.psum_scatter(jnp.einsum('tcji,tif->cjf', selected, row_grad, preferre...]
    ppermute x0 -> x10, starting transfers between devices: none -> 24.7 us  [_allreduce_doubling(): lax.ppermute(x, ('blk', 'rep'), [(i, i ^ mask) for i in range(total)])]
  transfers between devices with their start and end apart: 3 -> 12, of which waited for: 3 -> 11; matrix products, arithmetic and copies ran while one was open for 3% -> 8% of each run, Pallas kernels for 0% -> 0%
where the time goes in v1:
time: 217 us; the launch traced here: 213 us
  waiting for transfers between devices  156 us (72%)
  starting transfers between devices  24.7 us (11%)
  between operations  14.2 us (7%)
  matrix products  9.72 us (4%)
  local copies, waits for them, and re-layouts  4.24 us (2%)
  other arithmetic  4.11 us (2%)
    ppermute x10, waiting for transfers between devices, _allreduce_doubling(): lax.ppermute(x, ('blk', 'rep'), [(i, i ^ mask) for i in range(total)])  104 us
    all_gather x1, waiting for transfers between devices, per_device(): gathered = lax.all_gather(features, 'blk', axis=0, tiled=True)  51.7 us
    ppermute x10, starting transfers between devices, _allreduce_doubling(): lax.ppermute(x, ('blk', 'rep'), [(i, i ^ mask) for i in range(total)])  24.7 us
  transfers between devices with their start and end apart: 12, of which 11 were waited for; matrix products, arithmetic and copies ran while one was open for 8% of the time, Pallas kernels for 0%

profile of v1, /device:TPU:15, one launch (start us, length us, event | category | flops | bytes accessed | tf_op | source)
XLA Modules:
  0.0 213.1 jit_solution(5158298634879784097)
XLA Ops:
  12.0 3.3 %convolution_bitcast_fusion = f32[32,128,256]{2,1,0:T(8,128)} fusion(bf16[2,128,256,1]{2,1,0,3:T(8,128)(2,1)S(1)} %bitcast.34, bf16[2,32,128,128]{3,1,2,0:T(8,128)(2,1)S(1)} %fusion.3), kind=kOutput, calls=%fused_computation.5 | convolution fusion | flops 536870912 | bytes 6422528 | tf_op jit(solution)/shard_map/tcji,tif->cjf/dot_general | solution.py:45
  15.4 51.7 %all-gather.2.cloned.1.call-done = bf16[32,128,256]{2,1,0:T(8,128)(2,1)} async-done(((bf16[2,128,256]{2,1,0:T(8,128)(2,1)}), bf16[32,128,256]{2,1,0:T(8,128)(2,1)}) %all-gather.2.cloned.1.call-update) | async-done | bytes 2097168 | tf_op jit(solution)/shard_map/all_gather | solution.py:24
  67.1 4.1 %gather_fusion = bf16[48,128,256]{2,1,0:T(8,128)(2,1)} fusion(bf16[32,128,256]{2,1,0:T(8,128)(2,1)} %all-gather.2.cloned.1.call-done, s32[1024]{0:T(1024)S(1)} %pad_clamp_fusion), kind=kCustom, calls=%fused_computation | custom fusion | bytes 6291648 | tf_op jit(solution)/shard_map/gather | solution.py:25
  71.2 2.8 %fusion.10 = bf16[2,256,128]{1,2,0:T(8,128)(2,1)S(1)} fusion(bf16[2,24,128,128]{3,2,1,0:T(8,128)(2,1)S(1)} %copy-done, bf16[2,24,128,256]{3,2,1,0:T(8,128)(2,1)} %bitcast.33, pred[2,24]{1,0:T(4,128)(4,1)S(1)} %iota_compare_fusion.1), kind=kOutput, calls=%fused_computation.14 | convolution fusion | flops 404291584 | bytes 4849712 | tf_op jit(solution)/shard_map/tsji,tsjf->tif/dot_general | solution.py:27
  74.3 2.2 %collective-permute-start = (f32[256,256]{1,0:T(8,128)S(1)}, f32[256,256]{1,0:T(8,128)S(1)}, u32[]{:S(2)}, u32[]{:S(2)}) collective-permute-start(f32[256,256]{1,0:T(8,128)S(1)} %convolution_bitcast_fusion.1), channel_id=1, source_target_pairs={{0,64},{1,65},{2,66},{3,67},{4,68},{5,69},{6,70},{7,71},{8,72},{9,... | collective-permute-start | bytes 786440 | tf_op jit(solution)/shard_map/ppermute | solution.py:63
  77.7 1.9 collective-permute-start.1
  79.7 7.6 %collective-permute-done.1 = f32[256,256]{1,0:T(8,128)S(1)} collective-permute-done((f32[256,256]{1,0:T(8,128)S(1)}, f32[256,256]{1,0:T(8,128)S(1)}, u32[]{:S(2)}, u32[]{:S(2)}) %collective-permute-start.1) | collective-permute-done | bytes 262176 | tf_op jit(solution)/shard_map/ppermute | solution.py:63
  87.3 2.8 %collective-permute-start.2 = (f32[256,256]{1,0:T(8,128)S(1)}, f32[256,256]{1,0:T(8,128)S(1)}, u32[]{:S(2)}, u32[]{:S(2)}) collective-permute-start(f32[256,256]{1,0:T(8,128)S(1)} %add.53), channel_id=1, source_target_pairs={{0,2},{1,3},{2,0},{3,1},{4,6},{5,7},{6,4},{7,5},{8,10},{9,11},{10,... | collective-permute-start | bytes 786440 | tf_op jit(solution)/shard_map/ppermute | solution.py:63
  90.1 13.7 %collective-permute-done.2 = f32[256,256]{1,0:T(8,128)S(1)} collective-permute-done((f32[256,256]{1,0:T(8,128)S(1)}, f32[256,256]{1,0:T(8,128)S(1)}, u32[]{:S(2)}, u32[]{:S(2)}) %collective-permute-start.2) | collective-permute-done | bytes 262176 | tf_op jit(solution)/shard_map/ppermute | solution.py:63
  103.8 6.0 %collective-permute-start.3 = (f32[256,256]{1,0:T(8,128)S(1)}, f32[256,256]{1,0:T(8,128)S(1)}, u32[]{:S(2)}, u32[]{:S(2)}) collective-permute-start(f32[256,256]{1,0:T(8,128)S(1)} %add.54), channel_id=1, source_target_pairs={{0,4},{1,5},{2,6},{3,7},{4,0},{5,1},{6,2},{7,3},{8,12},{9,13},{10,... | collective-permute-start | bytes 786440 | tf_op jit(solution)/shard_map/ppermute | solution.py:63
  109.8 12.8 %collective-permute-done.3 = f32[256,256]{1,0:T(8,128)S(1)} collective-permute-done((f32[256,256]{1,0:T(8,128)S(1)}, f32[256,256]{1,0:T(8,128)S(1)}, u32[]{:S(2)}, u32[]{:S(2)}) %collective-permute-start.3) | collective-permute-done | bytes 262176 | tf_op jit(solution)/shard_map/ppermute | solution.py:63
  122.6 2.1 collective-permute-start.4
  124.7 6.5 %collective-permute-done.4 = f32[256,256]{1,0:T(8,128)S(1)} collective-permute-done((f32[256,256]{1,0:T(8,128)S(1)}, f32[256,256]{1,0:T(8,128)S(1)}, u32[]{:S(2)}, u32[]{:S(2)}) %collective-permute-start.4) | collective-permute-done | bytes 262176 | tf_op jit(solution)/shard_map/ppermute | solution.py:63
  131.2 2.1 collective-permute-start.5
  133.3 13.9 %collective-permute-done.5 = f32[256,256]{1,0:T(8,128)S(1)} collective-permute-done((f32[256,256]{1,0:T(8,128)S(1)}, f32[256,256]{1,0:T(8,128)S(1)}, u32[]{:S(2)}, u32[]{:S(2)}) %collective-permute-start.5) | collective-permute-done | bytes 262176 | tf_op jit(solution)/shard_map/ppermute | solution.py:63
  147.3 1.9 collective-permute-start.6
  149.2 13.9 %collective-permute-done.6 = f32[256,256]{1,0:T(8,128)S(1)} collective-permute-done((f32[256,256]{1,0:T(8,128)S(1)}, f32[256,256]{1,0:T(8,128)S(1)}, u32[]{:S(2)}, u32[]{:S(2)}) %collective-permute-start.6) | collective-permute-done | bytes 262176 | tf_op jit(solution)/shard_map/ppermute | solution.py:63
  163.1 1.9 collective-permute-start.7
  165.1 6.2 %collective-permute-done.7 = f32[256,256]{1,0:T(8,128)S(1)} collective-permute-done((f32[256,256]{1,0:T(8,128)S(1)}, f32[256,256]{1,0:T(8,128)S(1)}, u32[]{:S(2)}, u32[]{:S(2)}) %collective-permute-start.7) | collective-permute-done | bytes 262176 | tf_op jit(solution)/shard_map/ppermute | solution.py:63
  171.3 1.9 collective-permute-start.8
  173.3 14.7 %collective-permute-done.8 = f32[256,256]{1,0:T(8,128)S(1)} collective-permute-done((f32[256,256]{1,0:T(8,128)S(1)}, f32[256,256]{1,0:T(8,128)S(1)}, u32[]{:S(2)}, u32[]{:S(2)}) %collective-permute-start.8) | collective-permute-done | bytes 262176 | tf_op jit(solution)/shard_map/ppermute | solution.py:63
  188.0 1.9 collective-permute-start.9
  190.8 13.0 %collective-permute-done.9 = f32[256,256]{1,0:T(8,128)S(1)} collective-permute-done((f32[256,256]{1,0:T(8,128)S(1)}, f32[256,256]{1,0:T(8,128)S(1)}, u32[]{:S(2)}, u32[]{:S(2)}) %collective-permute-start.9) | collective-permute-done | bytes 262176 | tf_op jit(solution)/shard_map/ppermute | solution.py:63
  204.6 1.6 multiply_convert_fusion
  (32 shorter events, 8.2 us)
Async XLA Ops:
  7.2 3.4 %copy-start = (bf16[2,24,128,128]{3,2,1,0:T(8,128)(2,1)S(1)}, bf16[2,24,128,128]{3,2,1,0:T(8,128)(2,1)}, u32[]{:S(2)}) copy-start(bf16[2,24,128,128]{3,2,1,0:T(8,128)(2,1)} %param.9) | copy-start | bytes 4718596
  7.2 59.9 %all-gather.2.cloned.1.call-start = ((), (), s32[]{:S(2)}) async-start(), calls=%async_computation.1 | async-start | bytes 2228224 | tf_op jit(solution)/shard_map/all_gather | solution.py:24
  7.9 196.7 %reduce-scatter.2.cloned.1.call-start = ((), (), s32[]{:S(2)}) async-start(), calls=%async_computation.2 | async-start | bytes 4456448 | tf_op jit(solution)/shard_map/reduce_scatter | solution.py:44
  71.2 2.8 %copy-start.2 = (bf16[2,128,256]{2,1,0:T(8,128)(2,1)S(1)}, bf16[2,128,256]{2,1,0:T(8,128)(2,1)}, u32[]{:S(2)}) copy-start(bf16[2,128,256]{2,1,0:T(8,128)(2,1)} %param.12) | copy-start | bytes 393220
  74.3 3.4 %collective-permute-start = (f32[256,256]{1,0:T(8,128)S(1)}, f32[256,256]{1,0:T(8,128)S(1)}, u32[]{:S(2)}, u32[]{:S(2)}) collective-permute-start(f32[256,256]{1,0:T(8,128)S(1)} %convolution_bitcast_fusion.1), channel_id=1, source_target_pairs={{0,64},{1,65},{2,66},{3,67},{4,68},{5,69},{6,70},{7,71},{8,72},{9,... | collective-permute-start | bytes 786440 | tf_op jit(solution)/shard_map/ppermute | solution.py:63
  77.7 9.5 %collective-permute-start.1 = (f32[256,256]{1,0:T(8,128)S(1)}, f32[256,256]{1,0:T(8,128)S(1)}, u32[]{:S(2)}, u32[]{:S(2)}) collective-permute-start(f32[256,256]{1,0:T(8,128)S(1)} %add.52), channel_id=1, source_target_pairs={{0,1},{1,0},{2,3},{3,2},{4,5},{5,4},{6,7},{7,6},{8,9},{9,8},{10,11... | collective-permute-start | bytes 786440 | tf_op jit(solution)/shard_map/ppermute | solution.py:63
  87.3 16.5 %collective-permute-start.2 = (f32[256,256]{1,0:T(8,128)S(1)}, f32[256,256]{1,0:T(8,128)S(1)}, u32[]{:S(2)}, u32[]{:S(2)}) collective-permute-start(f32[256,256]{1,0:T(8,128)S(1)} %add.53), channel_id=1, source_target_pairs={{0,2},{1,3},{2,0},{3,1},{4,6},{5,7},{6,4},{7,5},{8,10},{9,11},{10,... | collective-permute-start | bytes 786440 | tf_op jit(solution)/shard_map/ppermute | solution.py:63
  103.8 18.8 %collective-permute-start.3 = (f32[256,256]{1,0:T(8,128)S(1)}, f32[256,256]{1,0:T(8,128)S(1)}, u32[]{:S(2)}, u32[]{:S(2)}) collective-permute-start(f32[256,256]{1,0:T(8,128)S(1)} %add.54), channel_id=1, source_target_pairs={{0,4},{1,5},{2,6},{3,7},{4,0},{5,1},{6,2},{7,3},{8,12},{9,13},{10,... | collective-permute-start | bytes 786440 | tf_op jit(solution)/shard_map/ppermute | solution.py:63
  122.6 67.3 %copy-start.1 = (bf16[256,256]{1,0:T(8,128)(2,1)S(1)}, bf16[256,256]{1,0:T(8,128)(2,1)}, u32[]{:S(2)}) copy-start(bf16[256,256]{1,0:T(8,128)(2,1)} %param.8) | copy-start | bytes 393220
  122.6 8.6 %collective-permute-start.4 = (f32[256,256]{1,0:T(8,128)S(1)}, f32[256,256]{1,0:T(8,128)S(1)}, u32[]{:S(2)}, u32[]{:S(2)}) collective-permute-start(f32[256,256]{1,0:T(8,128)S(1)} %add.55), channel_id=1, source_target_pairs={{0,8},{1,9},{2,10},{3,11},{4,12},{5,13},{6,14},{7,15},{8,0},{9,1},... | collective-permute-start | bytes 786440 | tf_op jit(solution)/shard_map/ppermute | solution.py:63
  131.2 73.4 %copy-start.3 = (s32[2,128,256]{2,1,0:T(8,128)S(1)}, s32[2,128,256]{2,1,0:T(8,128)}, u32[]{:S(2)}) copy-start(s32[2,128,256]{2,1,0:T(8,128)} %param.13) | copy-start | bytes 786436
  131.2 16.0 %collective-permute-start.5 = (f32[256,256]{1,0:T(8,128)S(1)}, f32[256,256]{1,0:T(8,128)S(1)}, u32[]{:S(2)}, u32[]{:S(2)}) collective-permute-start(f32[256,256]{1,0:T(8,128)S(1)} %add.56), channel_id=1, source_target_pairs={{0,16},{1,17},{2,18},{3,19},{4,20},{5,21},{6,22},{7,23},{8,24},{9,... | collective-permute-start | bytes 786440 | tf_op jit(solution)/shard_map/ppermute | solution.py:63
  147.3 15.8 %collective-permute-start.6 = (f32[256,256]{1,0:T(8,128)S(1)}, f32[256,256]{1,0:T(8,128)S(1)}, u32[]{:S(2)}, u32[]{:S(2)}) collective-permute-start(f32[256,256]{1,0:T(8,128)S(1)} %add.57), channel_id=1, source_target_pairs={{0,32},{1,33},{2,34},{3,35},{4,36},{5,37},{6,38},{7,39},{8,40},{9,... | collective-permute-start | bytes 786440 | tf_op jit(solution)/shard_map/ppermute | solution.py:63
  163.1 8.2 %collective-permute-start.7 = (f32[256,256]{1,0:T(8,128)S(1)}, f32[256,256]{1,0:T(8,128)S(1)}, u32[]{:S(2)}, u32[]{:S(2)}) collective-permute-start(f32[256,256]{1,0:T(8,128)S(1)} %add.58), channel_id=1, source_target_pairs={{0,128},{1,129},{2,130},{3,131},{4,132},{5,133},{6,134},{7,135},{8... | collective-permute-start | bytes 786440 | tf_op jit(solution)/shard_map/ppermute | solution.py:63
  171.3 16.7 %collective-permute-start.8 = (f32[256,256]{1,0:T(8,128)S(1)}, f32[256,256]{1,0:T(8,128)S(1)}, u32[]{:S(2)}, u32[]{:S(2)}) collective-permute-start(f32[256,256]{1,0:T(8,128)S(1)} %add.59), channel_id=1, source_target_pairs={{0,256},{1,257},{2,258},{3,259},{4,260},{5,261},{6,262},{7,263},{8... | collective-permute-start | bytes 786440 | tf_op jit(solution)/shard_map/ppermute | solution.py:63
  188.0 15.8 %collective-permute-start.9 = (f32[256,256]{1,0:T(8,128)S(1)}, f32[256,256]{1,0:T(8,128)S(1)}, u32[]{:S(2)}, u32[]{:S(2)}) collective-permute-start(f32[256,256]{1,0:T(8,128)S(1)} %add.60), channel_id=1, source_target_pairs={{0,512},{1,513},{2,514},{3,515},{4,516},{5,517},{6,518},{7,519},{8... | collective-permute-start | bytes 786440 | tf_op jit(solution)/shard_map/ppermute | solution.py:63
Sparse Core Ops, SparseCore 0:
  10.7 56.3 all-gather.1
  70.5 67.4 reduce-scatter.1

commit v2 on v1

--- a/solution.py
+++ b/solution.py
@@ -59,9 +59,19 @@
 
 def _allreduce_doubling(x, blk_size, rep_size):
     total = blk_size * rep_size
-    for mask in _bits_order(blk_size, rep_size):
-        x = x + lax.ppermute(x, ("blk", "rep"), [(i, i ^ mask) for i in range(total)])
-    return x
+    me = lax.axis_index(("blk", "rep"))
+    masks = _bits_order(blk_size, rep_size)
+    flat = x.reshape(-1)
+    half = flat.shape[0] // 2
+    upper = (me & masks[0]) != 0
+    keep = jnp.where(upper, flat[half:], flat[:half])
+    send = jnp.where(upper, flat[:half], flat[half:])
+    flat = keep + lax.ppermute(send, ("blk", "rep"), [(i, i ^ masks[0]) for i in range(total)])
+    for mask in masks[1:]:
+        flat = flat + lax.ppermute(flat, ("blk", "rep"), [(i, i ^ mask) for i in range(total)])
+    other = lax.ppermute(flat, ("blk", "rep"), [(i, i ^ masks[0]) for i in range(total)])
+    flat = jnp.concatenate([jnp.where(upper, other, flat), jnp.where(upper, flat, other)])
+    return flat.reshape(x.shape)
 
 
 def _allreduce_halving(x, blk_size, rep_size):

time: 217 us -> 185 us (0.85)
  waiting for transfers between devices: 156 us -> 108 us
  starting transfers between devices: 24.7 us -> 41.4 us
    ppermute x10 -> x11, waiting for transfers between devices: 104 us -> 55.9 us  [the longest x9 54.8 us: _allreduce_doubling(): lax.ppermute(flat, ('blk', 'rep'), [(i, i ^ mask) for i in range(total)])]
    ppermute x10 -> x11, starting transfers between devices: 24.7 us -> 41.4 us  [the longest x9 24.9 us: _allreduce_doubling(): lax.ppermute(flat, ('blk', 'rep'), [(i, i ^ mask) for i in range(total)])]
  transfers between devices with their start and end apart: 12 -> 13, of which waited for: 11 -> 12; matrix products, arithmetic and copies ran while one was open for 8% -> 9% of each run, Pallas kernels for 0% -> 0%
where the time goes in v2:
time: 185 us; the launch traced here: 182 us
  waiting for transfers between devices  108 us (58%)
  starting transfers between devices  41.4 us (22%)
  between operations  14.3 us (8%)
  matrix products  9.71 us (5%)
  local copies, waits for them, and re-layouts  4.46 us (2%)
  other arithmetic  3.99 us (2%)
    ppermute x9, waiting for transfers between devices, _allreduce_doubling(): lax.ppermute(flat, ('blk', 'rep'), [(i, i ^ mask) for i in range(total)])  54.8 us
    all_gather x1, waiting for transfers between devices, per_device(): gathered = lax.all_gather(features, 'blk', axis=0, tiled=True)  51.7 us
    ppermute x9, starting transfers between devices, _allreduce_doubling(): lax.ppermute(flat, ('blk', 'rep'), [(i, i ^ mask) for i in range(total)])  24.9 us
    ppermute x1, starting transfers between devices, _allreduce_doubling(): lax.ppermute(flat, ('blk', 'rep'), [(i, i ^ masks[0]) for i in range(tota...  14.3 us
    gather x1, local copies, waits for them, and re-layouts, per_device(): picked = gathered[local_cols]  4.14 us
  transfers between devices with their start and end apart: 13, of which 12 were waited for; matrix products, arithmetic and copies ran while one was open for 9% of the time, Pallas kernels for 0%

profile of v2, /device:TPU:15, one launch (start us, length us, event | category | flops | bytes accessed | tf_op | source)
XLA Modules:
  0.0 182.2 jit_solution(10735911834141616356)
XLA Ops:
  12.0 3.3 %convolution_bitcast_fusion = f32[32,128,256]{2,1,0:T(8,128)} fusion(bf16[2,128,256,1]{2,1,0,3:T(8,128)(2,1)S(1)} %bitcast.40, bf16[2,32,128,128]{3,1,2,0:T(8,128)(2,1)S(1)} %fusion.3), kind=kOutput, calls=%fused_computation.5 | convolution fusion | flops 536870912 | bytes 6422528 | tf_op jit(solution)/shard_map/tcji,tif->cjf/dot_general | solution.py:45
  15.4 51.7 %all-gather.2.cloned.1.call-done = bf16[32,128,256]{2,1,0:T(8,128)(2,1)} async-done(((bf16[2,128,256]{2,1,0:T(8,128)(2,1)}), bf16[32,128,256]{2,1,0:T(8,128)(2,1)}) %all-gather.2.cloned.1.call-update) | async-done | bytes 2097168 | tf_op jit(solution)/shard_map/all_gather | solution.py:24
  67.1 4.1 %gather_fusion = bf16[48,128,256]{2,1,0:T(8,128)(2,1)} fusion(bf16[32,128,256]{2,1,0:T(8,128)(2,1)} %all-gather.2.cloned.1.call-done, s32[1024]{0:T(1024)S(1)} %pad_clamp_fusion), kind=kCustom, calls=%fused_computation | custom fusion | bytes 6291648 | tf_op jit(solution)/shard_map/gather | solution.py:25
  71.2 2.8 %fusion.10 = bf16[2,256,128]{1,2,0:T(8,128)(2,1)S(1)} fusion(bf16[2,24,128,128]{3,2,1,0:T(8,128)(2,1)S(1)} %copy-done, bf16[2,24,128,256]{3,2,1,0:T(8,128)(2,1)} %bitcast.39, pred[2,24]{1,0:T(4,128)(4,1)S(1)} %iota_compare_fusion.1), kind=kOutput, calls=%fused_computation.14 | convolution fusion | flops 404291584 | bytes 4849712 | tf_op jit(solution)/shard_map/tsji,tsjf->tif/dot_general | solution.py:27
  74.4 2.2 %collective-permute-start = (f32[32768]{0:T(1024)S(1)}, f32[32768]{0:T(1024)S(1)}, u32[]{:S(2)}, u32[]{:S(2)}) collective-permute-start(f32[32768]{0:T(1024)S(1)} %bitcast.45), channel_id=1, source_target_pairs={{0,64},{1,65},{2,66},{3,67},{4,68},{5,69},{6,70},{7,71},{8,72},{9,... | collective-permute-start | bytes 393224 | tf_op jit(solution)/shard_map/ppermute | solution.py:69
  77.6 1.9 %collective-permute-start.1 = (f32[32768]{0:T(1024)S(1)}, f32[32768]{0:T(1024)S(1)}, u32[]{:S(2)}, u32[]{:S(2)}) collective-permute-start(f32[32768]{0:T(1024)S(1)} %add.56), channel_id=1, source_target_pairs={{0,1},{1,0},{2,3},{3,2},{4,5},{5,4},{6,7},{7,6},{8,9},{9,8},{10,11... | collective-permute-start | bytes 393224 | tf_op jit(solution)/shard_map/ppermute | solution.py:71
  79.6 4.8 %collective-permute-done.1 = f32[32768]{0:T(1024)S(1)} collective-permute-done((f32[32768]{0:T(1024)S(1)}, f32[32768]{0:T(1024)S(1)}, u32[]{:S(2)}, u32[]{:S(2)}) %collective-permute-start.1) | collective-permute-done | bytes 131104 | tf_op jit(solution)/shard_map/ppermute | solution.py:71
  84.4 2.8 %collective-permute-start.2 = (f32[32768]{0:T(1024)S(1)}, f32[32768]{0:T(1024)S(1)}, u32[]{:S(2)}, u32[]{:S(2)}) collective-permute-start(f32[32768]{0:T(1024)S(1)} %add.57), channel_id=1, source_target_pairs={{0,2},{1,3},{2,0},{3,1},{4,6},{5,7},{6,4},{7,5},{8,10},{9,11},{10,... | collective-permute-start | bytes 393224 | tf_op jit(solution)/shard_map/ppermute | solution.py:71
  87.1 8.1 %collective-permute-done.2 = f32[32768]{0:T(1024)S(1)} collective-permute-done((f32[32768]{0:T(1024)S(1)}, f32[32768]{0:T(1024)S(1)}, u32[]{:S(2)}, u32[]{:S(2)}) %collective-permute-start.2) | collective-permute-done | bytes 131104 | tf_op jit(solution)/shard_map/ppermute | solution.py:71
  95.2 6.0 %collective-permute-start.3 = (f32[32768]{0:T(1024)S(1)}, f32[32768]{0:T(1024)S(1)}, u32[]{:S(2)}, u32[]{:S(2)}) collective-permute-start(f32[32768]{0:T(1024)S(1)} %add.58), channel_id=1, source_target_pairs={{0,4},{1,5},{2,6},{3,7},{4,0},{5,1},{6,2},{7,3},{8,12},{9,13},{10,... | collective-permute-start | bytes 393224 | tf_op jit(solution)/shard_map/ppermute | solution.py:71
  101.2 7.2 %collective-permute-done.3 = f32[32768]{0:T(1024)S(1)} collective-permute-done((f32[32768]{0:T(1024)S(1)}, f32[32768]{0:T(1024)S(1)}, u32[]{:S(2)}, u32[]{:S(2)}) %collective-permute-start.3) | collective-permute-done | bytes 131104 | tf_op jit(solution)/shard_map/ppermute | solution.py:71
  108.4 2.1 %collective-permute-start.4 = (f32[32768]{0:T(1024)S(1)}, f32[32768]{0:T(1024)S(1)}, u32[]{:S(2)}, u32[]{:S(2)}) collective-permute-start(f32[32768]{0:T(1024)S(1)} %add.59), channel_id=1, source_target_pairs={{0,8},{1,9},{2,10},{3,11},{4,12},{5,13},{6,14},{7,15},{8,0},{9,1},... | collective-permute-start | bytes 393224 | tf_op jit(solution)/shard_map/ppermute | solution.py:71
  110.5 3.8 %collective-permute-done.4 = f32[32768]{0:T(1024)S(1)} collective-permute-done((f32[32768]{0:T(1024)S(1)}, f32[32768]{0:T(1024)S(1)}, u32[]{:S(2)}, u32[]{:S(2)}) %collective-permute-start.4) | collective-permute-done | bytes 131104 | tf_op jit(solution)/shard_map/ppermute | solution.py:71
  114.3 1.9 %collective-permute-start.5 = (f32[32768]{0:T(1024)S(1)}, f32[32768]{0:T(1024)S(1)}, u32[]{:S(2)}, u32[]{:S(2)}) collective-permute-start(f32[32768]{0:T(1024)S(1)} %add.60), channel_id=1, source_target_pairs={{0,16},{1,17},{2,18},{3,19},{4,20},{5,21},{6,22},{7,23},{8,24},{9,... | collective-permute-start | bytes 393224 | tf_op jit(solution)/shard_map/ppermute | solution.py:71
  116.2 5.8 %collective-permute-done.5 = f32[32768]{0:T(1024)S(1)} collective-permute-done((f32[32768]{0:T(1024)S(1)}, f32[32768]{0:T(1024)S(1)}, u32[]{:S(2)}, u32[]{:S(2)}) %collective-permute-start.5) | collective-permute-done | bytes 131104 | tf_op jit(solution)/shard_map/ppermute | solution.py:71
  122.1 4.5 %collective-permute-start.6 = (f32[32768]{0:T(1024)S(1)}, f32[32768]{0:T(1024)S(1)}, u32[]{:S(2)}, u32[]{:S(2)}) collective-permute-start(f32[32768]{0:T(1024)S(1)} %add.61), channel_id=1, source_target_pairs={{0,32},{1,33},{2,34},{3,35},{4,36},{5,37},{6,38},{7,39},{8,40},{9,... | collective-permute-start | bytes 393224 | tf_op jit(solution)/shard_map/ppermute | solution.py:71
  126.6 6.6 %collective-permute-done.6 = f32[32768]{0:T(1024)S(1)} collective-permute-done((f32[32768]{0:T(1024)S(1)}, f32[32768]{0:T(1024)S(1)}, u32[]{:S(2)}, u32[]{:S(2)}) %collective-permute-start.6) | collective-permute-done | bytes 131104 | tf_op jit(solution)/shard_map/ppermute | solution.py:71
  133.1 1.9 %collective-permute-start.7 = (f32[32768]{0:T(1024)S(1)}, f32[32768]{0:T(1024)S(1)}, u32[]{:S(2)}, u32[]{:S(2)}) collective-permute-start(f32[32768]{0:T(1024)S(1)} %add.62), channel_id=1, source_target_pairs={{0,128},{1,129},{2,130},{3,131},{4,132},{5,133},{6,134},{7,135},{8... | collective-permute-start | bytes 393224 | tf_op jit(solution)/shard_map/ppermute | solution.py:71
  135.1 4.1 %collective-permute-done.7 = f32[32768]{0:T(1024)S(1)} collective-permute-done((f32[32768]{0:T(1024)S(1)}, f32[32768]{0:T(1024)S(1)}, u32[]{:S(2)}, u32[]{:S(2)}) %collective-permute-start.7) | collective-permute-done | bytes 131104 | tf_op jit(solution)/shard_map/ppermute | solution.py:71
  139.2 1.9 %collective-permute-start.8 = (f32[32768]{0:T(1024)S(1)}, f32[32768]{0:T(1024)S(1)}, u32[]{:S(2)}, u32[]{:S(2)}) collective-permute-start(f32[32768]{0:T(1024)S(1)} %add.63), channel_id=1, source_target_pairs={{0,256},{1,257},{2,258},{3,259},{4,260},{5,261},{6,262},{7,263},{8... | collective-permute-start | bytes 393224 | tf_op jit(solution)/shard_map/ppermute | solution.py:71
  141.1 5.9 %collective-permute-done.8 = f32[32768]{0:T(1024)S(1)} collective-permute-done((f32[32768]{0:T(1024)S(1)}, f32[32768]{0:T(1024)S(1)}, u32[]{:S(2)}, u32[]{:S(2)}) %collective-permute-start.8) | collective-permute-done | bytes 131104 | tf_op jit(solution)/shard_map/ppermute | solution.py:71
  147.0 1.9 %collective-permute-start.9 = (f32[32768]{0:T(1024)S(1)}, f32[32768]{0:T(1024)S(1)}, u32[]{:S(2)}, u32[]{:S(2)}) collective-permute-start(f32[32768]{0:T(1024)S(1)} %add.64), channel_id=1, source_target_pairs={{0,512},{1,513},{2,514},{3,515},{4,516},{5,517},{6,518},{7,519},{8... | collective-permute-start | bytes 393224 | tf_op jit(solution)/shard_map/ppermute | solution.py:71
  149.0 8.6 %collective-permute-done.9 = f32[32768]{0:T(1024)S(1)} collective-permute-done((f32[32768]{0:T(1024)S(1)}, f32[32768]{0:T(1024)S(1)}, u32[]{:S(2)}, u32[]{:S(2)}) %collective-permute-start.9) | collective-permute-done | bytes 131104 | tf_op jit(solution)/shard_map/ppermute | solution.py:71
  157.6 14.3 %collective-permute-start.10 = (f32[32768]{0:T(1024)S(1)}, f32[32768]{0:T(1024)S(1)}, u32[]{:S(2)}, u32[]{:S(2)}) collective-permute-start(f32[32768]{0:T(1024)S(1)} %add.65), channel_id=1, source_target_pairs={{0,64},{1,65},{2,66},{3,67},{4,68},{5,69},{6,70},{7,71},{8,72},{9,... | collective-permute-start | bytes 393224 | tf_op jit(solution)/shard_map/ppermute | solution.py:72
  (41 shorter events, 9.8 us)
Async XLA Ops:
  7.2 3.4 %copy-start = (bf16[2,24,128,128]{3,2,1,0:T(8,128)(2,1)S(1)}, bf16[2,24,128,128]{3,2,1,0:T(8,128)(2,1)}, u32[]{:S(2)}) copy-start(bf16[2,24,128,128]{3,2,1,0:T(8,128)(2,1)} %param.9) | copy-start | bytes 4718596
  7.2 59.9 %all-gather.2.cloned.1.call-start = ((), (), s32[]{:S(2)}) async-start(), calls=%async_computation.1 | async-start | bytes 2228224 | tf_op jit(solution)/shard_map/all_gather | solution.py:24
  7.9 165.8 %reduce-scatter.2.cloned.1.call-start = ((), (), s32[]{:S(2)}) async-start(), calls=%async_computation.2 | async-start | bytes 4456448 | tf_op jit(solution)/shard_map/reduce_scatter | solution.py:44
  71.2 2.8 %copy-start.2 = (bf16[2,128,256]{2,1,0:T(8,128)(2,1)S(1)}, bf16[2,128,256]{2,1,0:T(8,128)(2,1)}, u32[]{:S(2)}) copy-start(bf16[2,128,256]{2,1,0:T(8,128)(2,1)} %param.12) | copy-start | bytes 393220
  74.4 3.2 %collective-permute-start = (f32[32768]{0:T(1024)S(1)}, f32[32768]{0:T(1024)S(1)}, u32[]{:S(2)}, u32[]{:S(2)}) collective-permute-start(f32[32768]{0:T(1024)S(1)} %bitcast.45), channel_id=1, source_target_pairs={{0,64},{1,65},{2,66},{3,67},{4,68},{5,69},{6,70},{7,71},{8,72},{9,... | collective-permute-start | bytes 393224 | tf_op jit(solution)/shard_map/ppermute | solution.py:69
  76.6 95.3 %copy-start.1 = (bf16[256,256]{1,0:T(8,128)(2,1)S(1)}, bf16[256,256]{1,0:T(8,128)(2,1)}, u32[]{:S(2)}) copy-start(bf16[256,256]{1,0:T(8,128)(2,1)} %param.8) | copy-start | bytes 393220
  77.6 6.7 %collective-permute-start.1 = (f32[32768]{0:T(1024)S(1)}, f32[32768]{0:T(1024)S(1)}, u32[]{:S(2)}, u32[]{:S(2)}) collective-permute-start(f32[32768]{0:T(1024)S(1)} %add.56), channel_id=1, source_target_pairs={{0,1},{1,0},{2,3},{3,2},{4,5},{5,4},{6,7},{7,6},{8,9},{9,8},{10,11... | collective-permute-start | bytes 393224 | tf_op jit(solution)/shard_map/ppermute | solution.py:71
  84.4 10.8 %collective-permute-start.2 = (f32[32768]{0:T(1024)S(1)}, f32[32768]{0:T(1024)S(1)}, u32[]{:S(2)}, u32[]{:S(2)}) collective-permute-start(f32[32768]{0:T(1024)S(1)} %add.57), channel_id=1, source_target_pairs={{0,2},{1,3},{2,0},{3,1},{4,6},{5,7},{6,4},{7,5},{8,10},{9,11},{10,... | collective-permute-start | bytes 393224 | tf_op jit(solution)/shard_map/ppermute | solution.py:71
  95.2 13.2 %collective-permute-start.3 = (f32[32768]{0:T(1024)S(1)}, f32[32768]{0:T(1024)S(1)}, u32[]{:S(2)}, u32[]{:S(2)}) collective-permute-start(f32[32768]{0:T(1024)S(1)} %add.58), channel_id=1, source_target_pairs={{0,4},{1,5},{2,6},{3,7},{4,0},{5,1},{6,2},{7,3},{8,12},{9,13},{10,... | collective-permute-start | bytes 393224 | tf_op jit(solution)/shard_map/ppermute | solution.py:71
  108.4 65.3 %copy-start.3 = (s32[2,128,256]{2,1,0:T(8,128)S(1)}, s32[2,128,256]{2,1,0:T(8,128)}, u32[]{:S(2)}) copy-start(s32[2,128,256]{2,1,0:T(8,128)} %param.13) | copy-start | bytes 786436
  108.4 5.8 %collective-permute-start.4 = (f32[32768]{0:T(1024)S(1)}, f32[32768]{0:T(1024)S(1)}, u32[]{:S(2)}, u32[]{:S(2)}) collective-permute-start(f32[32768]{0:T(1024)S(1)} %add.59), channel_id=1, source_target_pairs={{0,8},{1,9},{2,10},{3,11},{4,12},{5,13},{6,14},{7,15},{8,0},{9,1},... | collective-permute-start | bytes 393224 | tf_op jit(solution)/shard_map/ppermute | solution.py:71
  114.3 7.7 %collective-permute-start.5 = (f32[32768]{0:T(1024)S(1)}, f32[32768]{0:T(1024)S(1)}, u32[]{:S(2)}, u32[]{:S(2)}) collective-permute-start(f32[32768]{0:T(1024)S(1)} %add.60), channel_id=1, source_target_pairs={{0,16},{1,17},{2,18},{3,19},{4,20},{5,21},{6,22},{7,23},{8,24},{9,... | collective-permute-start | bytes 393224 | tf_op jit(solution)/shard_map/ppermute | solution.py:71
  122.1 11.0 %collective-permute-start.6 = (f32[32768]{0:T(1024)S(1)}, f32[32768]{0:T(1024)S(1)}, u32[]{:S(2)}, u32[]{:S(2)}) collective-permute-start(f32[32768]{0:T(1024)S(1)} %add.61), channel_id=1, source_target_pairs={{0,32},{1,33},{2,34},{3,35},{4,36},{5,37},{6,38},{7,39},{8,40},{9,... | collective-permute-start | bytes 393224 | tf_op jit(solution)/shard_map/ppermute | solution.py:71
  133.1 6.0 %collective-permute-start.7 = (f32[32768]{0:T(1024)S(1)}, f32[32768]{0:T(1024)S(1)}, u32[]{:S(2)}, u32[]{:S(2)}) collective-permute-start(f32[32768]{0:T(1024)S(1)} %add.62), channel_id=1, source_target_pairs={{0,128},{1,129},{2,130},{3,131},{4,132},{5,133},{6,134},{7,135},{8... | collective-permute-start | bytes 393224 | tf_op jit(solution)/shard_map/ppermute | solution.py:71
  139.2 7.9 %collective-permute-start.8 = (f32[32768]{0:T(1024)S(1)}, f32[32768]{0:T(1024)S(1)}, u32[]{:S(2)}, u32[]{:S(2)}) collective-permute-start(f32[32768]{0:T(1024)S(1)} %add.63), channel_id=1, source_target_pairs={{0,256},{1,257},{2,258},{3,259},{4,260},{5,261},{6,262},{7,263},{8... | collective-permute-start | bytes 393224 | tf_op jit(solution)/shard_map/ppermute | solution.py:71
  147.0 10.6 %collective-permute-start.9 = (f32[32768]{0:T(1024)S(1)}, f32[32768]{0:T(1024)S(1)}, u32[]{:S(2)}, u32[]{:S(2)}) collective-permute-start(f32[32768]{0:T(1024)S(1)} %add.64), channel_id=1, source_target_pairs={{0,512},{1,513},{2,514},{3,515},{4,516},{5,517},{6,518},{7,519},{8... | collective-permute-start | bytes 393224 | tf_op jit(solution)/shard_map/ppermute | solution.py:71
  157.6 15.2 %collective-permute-start.10 = (f32[32768]{0:T(1024)S(1)}, f32[32768]{0:T(1024)S(1)}, u32[]{:S(2)}, u32[]{:S(2)}) collective-permute-start(f32[32768]{0:T(1024)S(1)} %add.65), channel_id=1, source_target_pairs={{0,64},{1,65},{2,66},{3,67},{4,68},{5,69},{6,70},{7,71},{8,72},{9,... | collective-permute-start | bytes 393224 | tf_op jit(solution)/shard_map/ppermute | solution.py:72
Sparse Core Ops, SparseCore 0:
  10.7 56.3 all-gather.1
  70.5 67.0 reduce-scatter.1

commit v3 on v1

--- a/solution.py
+++ b/solution.py
@@ -54,29 +54,26 @@
 def _bits_order(blk_size, rep_size):
     rep_bits = [1 << b for b in range(rep_size.bit_length() - 1)]
     blk_bits = [rep_size << b for b in range(blk_size.bit_length() - 1)]
-    return blk_bits[:1] + rep_bits + blk_bits[1:]
+    side = len(rep_bits) // 2
+    near = [blk_bits[0], rep_bits[0], rep_bits[side], blk_bits[1]]
+    far = rep_bits[1:side] + rep_bits[side + 1:] + blk_bits[2:]
+    return near[:2], near[2:] + far
 
 
 def _allreduce_doubling(x, blk_size, rep_size):
     total = blk_size * rep_size
-    for mask in _bits_order(blk_size, rep_size):
-        x = x + lax.ppermute(x, ("blk", "rep"), [(i, i ^ mask) for i in range(total)])
-    return x
-
-
-def _allreduce_halving(x, blk_size, rep_size):
-    total = blk_size * rep_size
     me = lax.axis_index(("blk", "rep"))
-    masks = _bits_order(blk_size, rep_size)
+    halving, doubling = _bits_order(blk_size, rep_size)
     flat = x.reshape(-1)
-    for mask in masks:
+    for mask in halving:
         half = flat.shape[0] // 2
         upper = (me & mask) != 0
-        lo, hi = flat[:half], flat[half:]
-        keep = jnp.where(upper, hi, lo)
-        send = jnp.where(upper, lo, hi)
+        keep = jnp.where(upper, flat[half:], flat[:half])
+        send = jnp.where(upper, flat[:half], flat[half:])
         flat = keep + lax.ppermute(send, ("blk", "rep"), [(i, i ^ mask) for i in range(total)])
-    for mask in reversed(masks):
+    for mask in doubling:
+        flat = flat + lax.ppermute(flat, ("blk", "rep"), [(i, i ^ mask) for i in range(total)])
+    for mask in reversed(halving):
         upper = (me & mask) != 0
         other = lax.ppermute(flat, ("blk", "rep"), [(i, i ^ mask) for i in range(total)])
         flat = jnp.concatenate([jnp.where(upper, other, flat), jnp.where(upper, flat, other)])

time: 217 us -> 172 us (0.79)
  waiting for transfers between devices: 156 us -> 79.9 us
  starting transfers between devices: 24.7 us -> 57.1 us
    ppermute x10 -> x12, waiting for transfers between devices: 104 us -> 27.5 us  [the longest x10 23.4 us: _allreduce_doubling(): lax.ppermute(flat, ('blk', 'rep'), [(i, i ^ mask) for i in range(total)])]
    ppermute x10 -> x12, starting transfers between devices: 24.7 us -> 57.1 us  [the longest x10 53 us: _allreduce_doubling(): lax.ppermute(flat, ('blk', 'rep'), [(i, i ^ mask) for i in range(total)])]
  transfers between devices with their start and end apart: 12 -> 14, of which waited for: 11 -> 13; matrix products, arithmetic and copies ran while one was open for 8% -> 10% of each run, Pallas kernels for 0% -> 0%
where the time goes in v3:
time: 172 us; the launch traced here: 169 us
  waiting for transfers between devices  79.9 us (46%)
  starting transfers between devices  57.1 us (33%)
  between operations  14.3 us (8%)
  matrix products  9.7 us (6%)
  local copies, waits for them, and re-layouts  4.45 us (3%)
  other arithmetic  3.96 us (2%)
    ppermute x10, starting transfers between devices, _allreduce_doubling(): lax.ppermute(flat, ('blk', 'rep'), [(i, i ^ mask) for i in range(total)])  53 us
    all_gather x1, waiting for transfers between devices, per_device(): gathered = lax.all_gather(features, 'blk', axis=0, tiled=True)  51.7 us
    ppermute x10, waiting for transfers between devices, _allreduce_doubling(): lax.ppermute(flat, ('blk', 'rep'), [(i, i ^ mask) for i in range(total)])  23.4 us
    gather x1, local copies, waits for them, and re-layouts, per_device(): picked = gathered[local_cols]  4.13 us
    ppermute x2, starting transfers between devices, _allreduce_doubling(): lax.ppermute(send, ('blk', 'rep'), [(i, i ^ mask) for i in range(total)])  4.11 us
    ppermute x2, waiting for transfers between devices, _allreduce_doubling(): lax.ppermute(send, ('blk', 'rep'), [(i, i ^ mask) for i in range(total)])  4.05 us
  transfers between devices with their start and end apart: 14, of which 13 were waited for; matrix products, arithmetic and copies ran while one was open for 10% of the time, Pallas kernels for 0%

profile of v3, /device:TPU:15, one launch (start us, length us, event | category | flops | bytes accessed | tf_op | source)
XLA Modules:
  0.0 169.5 jit_solution(16599866785557407613)
XLA Ops:
  12.0 3.3 %convolution_bitcast_fusion = f32[32,128,256]{2,1,0:T(8,128)} fusion(bf16[2,128,256,1]{2,1,0,3:T(8,128)(2,1)S(1)} %bitcast.40, bf16[2,32,128,128]{3,1,2,0:T(8,128)(2,1)S(1)} %fusion.3), kind=kOutput, calls=%fused_computation.5 | convolution fusion | flops 536870912 | bytes 6422528 | tf_op jit(solution)/shard_map/tcji,tif->cjf/dot_general | solution.py:45
  15.4 51.7 %all-gather.2.cloned.1.call-done = bf16[32,128,256]{2,1,0:T(8,128)(2,1)} async-done(((bf16[2,128,256]{2,1,0:T(8,128)(2,1)}), bf16[32,128,256]{2,1,0:T(8,128)(2,1)}) %all-gather.2.cloned.1.call-update) | async-done | bytes 2097168 | tf_op jit(solution)/shard_map/all_gather | solution.py:24
  67.1 4.1 %gather_fusion = bf16[48,128,256]{2,1,0:T(8,128)(2,1)} fusion(bf16[32,128,256]{2,1,0:T(8,128)(2,1)} %all-gather.2.cloned.1.call-done, s32[1024]{0:T(1024)S(1)} %pad_clamp_fusion), kind=kCustom, calls=%fused_computation | custom fusion | bytes 6291648 | tf_op jit(solution)/shard_map/gather | solution.py:25
  71.2 2.8 %fusion.10 = bf16[2,256,128]{1,2,0:T(8,128)(2,1)S(1)} fusion(bf16[2,24,128,128]{3,2,1,0:T(8,128)(2,1)S(1)} %copy-done, bf16[2,24,128,256]{3,2,1,0:T(8,128)(2,1)} %bitcast.39, pred[2,24]{1,0:T(4,128)(4,1)S(1)} %iota_compare_fusion.1), kind=kOutput, calls=%fused_computation.14 | convolution fusion | flops 404291584 | bytes 4849712 | tf_op jit(solution)/shard_map/tsji,tsjf->tif/dot_general | solution.py:27
  74.4 2.2 %collective-permute-start = (f32[32768]{0:T(1024)S(1)}, f32[32768]{0:T(1024)S(1)}, u32[]{:S(2)}, u32[]{:S(2)}) collective-permute-start(f32[32768]{0:T(1024)S(1)} %bitcast.45), channel_id=1, source_target_pairs={{0,64},{1,65},{2,66},{3,67},{4,68},{5,69},{6,70},{7,71},{8,72},{9,... | collective-permute-start | bytes 393224 | tf_op jit(solution)/shard_map/ppermute | solution.py:73
  77.7 1.9 %collective-permute-start.1 = (f32[16384]{0:T(1024)S(1)}, f32[16384]{0:T(1024)S(1)}, u32[]{:S(2)}, u32[]{:S(2)}) collective-permute-start(f32[16384]{0:T(1024)S(1)} %slice_select_fusion), channel_id=1, source_target_pairs={{0,1},{1,0},{2,3},{3,2},{4,5},{5,4},{6,7},{7,6},{8,9},{9,8},{10,11... | collective-permute-start | bytes 196616 | tf_op jit(solution)/shard_map/ppermute | solution.py:73
  79.6 3.1 %collective-permute-done.1 = f32[16384]{0:T(1024)S(1)} collective-permute-done((f32[16384]{0:T(1024)S(1)}, f32[16384]{0:T(1024)S(1)}, u32[]{:S(2)}, u32[]{:S(2)}) %collective-permute-start.1) | collective-permute-done | bytes 65568 | tf_op jit(solution)/shard_map/ppermute | solution.py:73
  82.7 2.3 %collective-permute-start.2 = (f32[16384]{0:T(1024)S(1)}, f32[16384]{0:T(1024)S(1)}, u32[]{:S(2)}, u32[]{:S(2)}) collective-permute-start(f32[16384]{0:T(1024)S(1)} %select_add_fusion), channel_id=1, source_target_pairs={{0,8},{1,9},{2,10},{3,11},{4,12},{5,13},{6,14},{7,15},{8,0},{9,1},... | collective-permute-start | bytes 196616 | tf_op jit(solution)/shard_map/ppermute | solution.py:75
  85.0 2.9 %collective-permute-done.2 = f32[16384]{0:T(1024)S(1)} collective-permute-done((f32[16384]{0:T(1024)S(1)}, f32[16384]{0:T(1024)S(1)}, u32[]{:S(2)}, u32[]{:S(2)}) %collective-permute-start.2) | collective-permute-done | bytes 65568 | tf_op jit(solution)/shard_map/ppermute | solution.py:75
  87.8 1.9 %collective-permute-start.3 = (f32[16384]{0:T(1024)S(1)}, f32[16384]{0:T(1024)S(1)}, u32[]{:S(2)}, u32[]{:S(2)}) collective-permute-start(f32[16384]{0:T(1024)S(1)} %add.58), channel_id=1, source_target_pairs={{0,128},{1,129},{2,130},{3,131},{4,132},{5,133},{6,134},{7,135},{8... | collective-permute-start | bytes 196616 | tf_op jit(solution)/shard_map/ppermute | solution.py:75
  89.8 3.1 %collective-permute-done.3 = f32[16384]{0:T(1024)S(1)} collective-permute-done((f32[16384]{0:T(1024)S(1)}, f32[16384]{0:T(1024)S(1)}, u32[]{:S(2)}, u32[]{:S(2)}) %collective-permute-start.3) | collective-permute-done | bytes 65568 | tf_op jit(solution)/shard_map/ppermute | solution.py:75
  92.9 3.9 %collective-permute-start.4 = (f32[16384]{0:T(1024)S(1)}, f32[16384]{0:T(1024)S(1)}, u32[]{:S(2)}, u32[]{:S(2)}) collective-permute-start(f32[16384]{0:T(1024)S(1)} %add.59), channel_id=1, source_target_pairs={{0,2},{1,3},{2,0},{3,1},{4,6},{5,7},{6,4},{7,5},{8,10},{9,11},{10,... | collective-permute-start | bytes 196616 | tf_op jit(solution)/shard_map/ppermute | solution.py:75
  96.7 2.0 %collective-permute-done.4 = f32[16384]{0:T(1024)S(1)} collective-permute-done((f32[16384]{0:T(1024)S(1)}, f32[16384]{0:T(1024)S(1)}, u32[]{:S(2)}, u32[]{:S(2)}) %collective-permute-start.4) | collective-permute-done | bytes 65568 | tf_op jit(solution)/shard_map/ppermute | solution.py:75
  98.8 7.7 %collective-permute-start.5 = (f32[16384]{0:T(1024)S(1)}, f32[16384]{0:T(1024)S(1)}, u32[]{:S(2)}, u32[]{:S(2)}) collective-permute-start(f32[16384]{0:T(1024)S(1)} %add.60), channel_id=1, source_target_pairs={{0,4},{1,5},{2,6},{3,7},{4,0},{5,1},{6,2},{7,3},{8,12},{9,13},{10,... | collective-permute-start | bytes 196616 | tf_op jit(solution)/shard_map/ppermute | solution.py:75
  108.2 4.7 %collective-permute-start.6 = (f32[16384]{0:T(1024)S(1)}, f32[16384]{0:T(1024)S(1)}, u32[]{:S(2)}, u32[]{:S(2)}) collective-permute-start(f32[16384]{0:T(1024)S(1)} %add.61), channel_id=1, source_target_pairs={{0,16},{1,17},{2,18},{3,19},{4,20},{5,21},{6,22},{7,23},{8,24},{9,... | collective-permute-start | bytes 196616 | tf_op jit(solution)/shard_map/ppermute | solution.py:75
  114.6 8.6 %collective-permute-start.7 = (f32[16384]{0:T(1024)S(1)}, f32[16384]{0:T(1024)S(1)}, u32[]{:S(2)}, u32[]{:S(2)}) collective-permute-start(f32[16384]{0:T(1024)S(1)} %add.62), channel_id=1, source_target_pairs={{0,32},{1,33},{2,34},{3,35},{4,36},{5,37},{6,38},{7,39},{8,40},{9,... | collective-permute-start | bytes 196616 | tf_op jit(solution)/shard_map/ppermute | solution.py:75
  123.2 2.2 %collective-permute-done.7 = f32[16384]{0:T(1024)S(1)} collective-permute-done((f32[16384]{0:T(1024)S(1)}, f32[16384]{0:T(1024)S(1)}, u32[]{:S(2)}, u32[]{:S(2)}) %collective-permute-start.7) | collective-permute-done | bytes 65568 | tf_op jit(solution)/shard_map/ppermute | solution.py:75
  125.4 3.7 %collective-permute-start.8 = (f32[16384]{0:T(1024)S(1)}, f32[16384]{0:T(1024)S(1)}, u32[]{:S(2)}, u32[]{:S(2)}) collective-permute-start(f32[16384]{0:T(1024)S(1)} %add.63), channel_id=1, source_target_pairs={{0,256},{1,257},{2,258},{3,259},{4,260},{5,261},{6,262},{7,263},{8... | collective-permute-start | bytes 196616 | tf_op jit(solution)/shard_map/ppermute | solution.py:75
  129.2 3.1 %collective-permute-done.8 = f32[16384]{0:T(1024)S(1)} collective-permute-done((f32[16384]{0:T(1024)S(1)}, f32[16384]{0:T(1024)S(1)}, u32[]{:S(2)}, u32[]{:S(2)}) %collective-permute-start.8) | collective-permute-done | bytes 65568 | tf_op jit(solution)/shard_map/ppermute | solution.py:75
  132.3 5.2 %collective-permute-start.9 = (f32[16384]{0:T(1024)S(1)}, f32[16384]{0:T(1024)S(1)}, u32[]{:S(2)}, u32[]{:S(2)}) collective-permute-start(f32[16384]{0:T(1024)S(1)} %add.64), channel_id=1, source_target_pairs={{0,512},{1,513},{2,514},{3,515},{4,516},{5,517},{6,518},{7,519},{8... | collective-permute-start | bytes 196616 | tf_op jit(solution)/shard_map/ppermute | solution.py:75
  137.5 4.3 %collective-permute-done.9 = f32[16384]{0:T(1024)S(1)} collective-permute-done((f32[16384]{0:T(1024)S(1)}, f32[16384]{0:T(1024)S(1)}, u32[]{:S(2)}, u32[]{:S(2)}) %collective-permute-start.9) | collective-permute-done | bytes 65568 | tf_op jit(solution)/shard_map/ppermute | solution.py:75
  141.8 2.7 %collective-permute-start.10 = (f32[16384]{0:T(1024)S(1)}, f32[16384]{0:T(1024)S(1)}, u32[]{:S(2)}, u32[]{:S(2)}) collective-permute-start(f32[16384]{0:T(1024)S(1)} %add.65), channel_id=1, source_target_pairs={{0,1},{1,0},{2,3},{3,2},{4,5},{5,4},{6,7},{7,6},{8,9},{9,8},{10,11... | collective-permute-start | bytes 196616 | tf_op jit(solution)/shard_map/ppermute | solution.py:78
  144.5 2.3 %collective-permute-done.10 = f32[16384]{0:T(1024)S(1)} collective-permute-done((f32[16384]{0:T(1024)S(1)}, f32[16384]{0:T(1024)S(1)}, u32[]{:S(2)}, u32[]{:S(2)}) %collective-permute-start.10) | collective-permute-done | bytes 65568 | tf_op jit(solution)/shard_map/ppermute | solution.py:78
  146.9 12.3 %collective-permute-start.11 = (f32[32768]{0:T(1024)S(1)}, f32[32768]{0:T(1024)S(1)}, u32[]{:S(2)}, u32[]{:S(2)}) collective-permute-start(f32[32768]{0:T(1024)S(1)} %pad_maximum_fusion), channel_id=1, source_target_pairs={{0,64},{1,65},{2,66},{3,67},{4,68},{5,69},{6,70},{7,71},{8,72},{9,... | collective-permute-start | bytes 393224 | tf_op jit(solution)/shard_map/ppermute | solution.py:78
  (46 shorter events, 13.1 us)
Async XLA Ops:
  7.2 3.4 %copy-start = (bf16[2,24,128,128]{3,2,1,0:T(8,128)(2,1)S(1)}, bf16[2,24,128,128]{3,2,1,0:T(8,128)(2,1)}, u32[]{:S(2)}) copy-start(bf16[2,24,128,128]{3,2,1,0:T(8,128)(2,1)} %param.9) | copy-start | bytes 4718596
  7.2 59.9 %all-gather.2.cloned.1.call-start = ((), (), s32[]{:S(2)}) async-start(), calls=%async_computation.1 | async-start | bytes 2228224 | tf_op jit(solution)/shard_map/all_gather | solution.py:24
  7.9 153.1 %reduce-scatter.2.cloned.1.call-start = ((), (), s32[]{:S(2)}) async-start(), calls=%async_computation.2 | async-start | bytes 4456448 | tf_op jit(solution)/shard_map/reduce_scatter | solution.py:44
  71.2 2.8 %copy-start.2 = (bf16[2,128,256]{2,1,0:T(8,128)(2,1)S(1)}, bf16[2,128,256]{2,1,0:T(8,128)(2,1)}, u32[]{:S(2)}) copy-start(bf16[2,128,256]{2,1,0:T(8,128)(2,1)} %param.12) | copy-start | bytes 393220
  74.3 84.9 %copy-start.1 = (bf16[256,256]{1,0:T(8,128)(2,1)S(1)}, bf16[256,256]{1,0:T(8,128)(2,1)}, u32[]{:S(2)}) copy-start(bf16[256,256]{1,0:T(8,128)(2,1)} %param.8) | copy-start | bytes 393220
  74.4 3.2 %collective-permute-start = (f32[32768]{0:T(1024)S(1)}, f32[32768]{0:T(1024)S(1)}, u32[]{:S(2)}, u32[]{:S(2)}) collective-permute-start(f32[32768]{0:T(1024)S(1)} %bitcast.45), channel_id=1, source_target_pairs={{0,64},{1,65},{2,66},{3,67},{4,68},{5,69},{6,70},{7,71},{8,72},{9,... | collective-permute-start | bytes 393224 | tf_op jit(solution)/shard_map/ppermute | solution.py:73
  77.7 5.0 %collective-permute-start.1 = (f32[16384]{0:T(1024)S(1)}, f32[16384]{0:T(1024)S(1)}, u32[]{:S(2)}, u32[]{:S(2)}) collective-permute-start(f32[16384]{0:T(1024)S(1)} %slice_select_fusion), channel_id=1, source_target_pairs={{0,1},{1,0},{2,3},{3,2},{4,5},{5,4},{6,7},{7,6},{8,9},{9,8},{10,11... | collective-permute-start | bytes 196616 | tf_op jit(solution)/shard_map/ppermute | solution.py:73
  82.7 78.3 %copy-start.3 = (s32[2,128,256]{2,1,0:T(8,128)S(1)}, s32[2,128,256]{2,1,0:T(8,128)}, u32[]{:S(2)}) copy-start(s32[2,128,256]{2,1,0:T(8,128)} %param.13) | copy-start | bytes 786436
  82.7 5.1 %collective-permute-start.2 = (f32[16384]{0:T(1024)S(1)}, f32[16384]{0:T(1024)S(1)}, u32[]{:S(2)}, u32[]{:S(2)}) collective-permute-start(f32[16384]{0:T(1024)S(1)} %select_add_fusion), channel_id=1, source_target_pairs={{0,8},{1,9},{2,10},{3,11},{4,12},{5,13},{6,14},{7,15},{8,0},{9,1},... | collective-permute-start | bytes 196616 | tf_op jit(solution)/shard_map/ppermute | solution.py:75
  87.8 5.0 %collective-permute-start.3 = (f32[16384]{0:T(1024)S(1)}, f32[16384]{0:T(1024)S(1)}, u32[]{:S(2)}, u32[]{:S(2)}) collective-permute-start(f32[16384]{0:T(1024)S(1)} %add.58), channel_id=1, source_target_pairs={{0,128},{1,129},{2,130},{3,131},{4,132},{5,133},{6,134},{7,135},{8... | collective-permute-start | bytes 196616 | tf_op jit(solution)/shard_map/ppermute | solution.py:75
  92.9 5.9 %collective-permute-start.4 = (f32[16384]{0:T(1024)S(1)}, f32[16384]{0:T(1024)S(1)}, u32[]{:S(2)}, u32[]{:S(2)}) collective-permute-start(f32[16384]{0:T(1024)S(1)} %add.59), channel_id=1, source_target_pairs={{0,2},{1,3},{2,0},{3,1},{4,6},{5,7},{6,4},{7,5},{8,10},{9,11},{10,... | collective-permute-start | bytes 196616 | tf_op jit(solution)/shard_map/ppermute | solution.py:75
  98.8 9.4 %collective-permute-start.5 = (f32[16384]{0:T(1024)S(1)}, f32[16384]{0:T(1024)S(1)}, u32[]{:S(2)}, u32[]{:S(2)}) collective-permute-start(f32[16384]{0:T(1024)S(1)} %add.60), channel_id=1, source_target_pairs={{0,4},{1,5},{2,6},{3,7},{4,0},{5,1},{6,2},{7,3},{8,12},{9,13},{10,... | collective-permute-start | bytes 196616 | tf_op jit(solution)/shard_map/ppermute | solution.py:75
  108.2 6.4 %collective-permute-start.6 = (f32[16384]{0:T(1024)S(1)}, f32[16384]{0:T(1024)S(1)}, u32[]{:S(2)}, u32[]{:S(2)}) collective-permute-start(f32[16384]{0:T(1024)S(1)} %add.61), channel_id=1, source_target_pairs={{0,16},{1,17},{2,18},{3,19},{4,20},{5,21},{6,22},{7,23},{8,24},{9,... | collective-permute-start | bytes 196616 | tf_op jit(solution)/shard_map/ppermute | solution.py:75
  114.6 10.8 %collective-permute-start.7 = (f32[16384]{0:T(1024)S(1)}, f32[16384]{0:T(1024)S(1)}, u32[]{:S(2)}, u32[]{:S(2)}) collective-permute-start(f32[16384]{0:T(1024)S(1)} %add.62), channel_id=1, source_target_pairs={{0,32},{1,33},{2,34},{3,35},{4,36},{5,37},{6,38},{7,39},{8,40},{9,... | collective-permute-start | bytes 196616 | tf_op jit(solution)/shard_map/ppermute | solution.py:75
  125.4 6.9 %collective-permute-start.8 = (f32[16384]{0:T(1024)S(1)}, f32[16384]{0:T(1024)S(1)}, u32[]{:S(2)}, u32[]{:S(2)}) collective-permute-start(f32[16384]{0:T(1024)S(1)} %add.63), channel_id=1, source_target_pairs={{0,256},{1,257},{2,258},{3,259},{4,260},{5,261},{6,262},{7,263},{8... | collective-permute-start | bytes 196616 | tf_op jit(solution)/shard_map/ppermute | solution.py:75
  132.3 9.5 %collective-permute-start.9 = (f32[16384]{0:T(1024)S(1)}, f32[16384]{0:T(1024)S(1)}, u32[]{:S(2)}, u32[]{:S(2)}) collective-permute-start(f32[16384]{0:T(1024)S(1)} %add.64), channel_id=1, source_target_pairs={{0,512},{1,513},{2,514},{3,515},{4,516},{5,517},{6,518},{7,519},{8... | collective-permute-start | bytes 196616 | tf_op jit(solution)/shard_map/ppermute | solution.py:75
  141.8 5.0 %collective-permute-start.10 = (f32[16384]{0:T(1024)S(1)}, f32[16384]{0:T(1024)S(1)}, u32[]{:S(2)}, u32[]{:S(2)}) collective-permute-start(f32[16384]{0:T(1024)S(1)} %add.65), channel_id=1, source_target_pairs={{0,1},{1,0},{2,3},{3,2},{4,5},{5,4},{6,7},{7,6},{8,9},{9,8},{10,11... | collective-permute-start | bytes 196616 | tf_op jit(solution)/shard_map/ppermute | solution.py:78
  146.9 13.3 %collective-permute-start.11 = (f32[32768]{0:T(1024)S(1)}, f32[32768]{0:T(1024)S(1)}, u32[]{:S(2)}, u32[]{:S(2)}) collective-permute-start(f32[32768]{0:T(1024)S(1)} %pad_maximum_fusion), channel_id=1, source_target_pairs={{0,64},{1,65},{2,66},{3,67},{4,68},{5,69},{6,70},{7,71},{8,72},{9,... | collective-permute-start | bytes 393224 | tf_op jit(solution)/shard_map/ppermute | solution.py:78
Sparse Core Ops, SparseCore 0:
  10.7 56.3 all-gather.1
  70.5 67.0 reduce-scatter.1

commit v4 on v3

--- a/solution.py
+++ b/solution.py
@@ -22,10 +22,8 @@
         "tsc,tsji->tcji", one_hot, tile_values, preferred_element_type=jnp.float32
     ).astype(jnp.bfloat16)
     gathered = lax.all_gather(features, "blk", axis=0, tiled=True)
-    picked = gathered[local_cols]
-    picked = jnp.where(in_use[:, :, None, None], picked, jnp.zeros((), jnp.bfloat16))
     partial_value = jnp.einsum(
-        "tsji,tsjf->tif", tile_values, picked, preferred_element_type=jnp.float32
+        "tcji,cjf->tif", selected, gathered, preferred_element_type=jnp.float32
     )
     hidden = partial_value.astype(jnp.bfloat16)
     hidden_flat = hidden.reshape(-1, feature_width)

time: 172 us -> 169 us (0.983)
  local copies, waits for them, and re-layouts: 4.45 us -> 1.61 us
  starting transfers between devices: 57.1 us -> 55 us
    gather x1 -> x0, local copies, waits for them, and re-layouts: 4.13 us -> none  [per_device(): picked = gathered[local_cols]]
    ppermute x10, waiting for transfers between devices: 23.4 us -> 26 us  [_allreduce_doubling(): lax.ppermute(flat, ('blk', 'rep'), [(i, i ^ mask) for i in range(total)])]
    ppermute x10, starting transfers between devices: 53 us -> 50.8 us  [_allreduce_doubling(): lax.ppermute(flat, ('blk', 'rep'), [(i, i ^ mask) for i in range(total)])]
  transfers between devices with their start and end apart: 14 -> 14, of which waited for: 13 -> 13; matrix products, arithmetic and copies ran while one was open for 10% -> 8% of each run, Pallas kernels for 0% -> 0%
where the time goes in v4:
time: 169 us; the launch traced here: 167 us
  waiting for transfers between devices  81.2 us (48%)
  starting transfers between devices  55 us (33%)
  between operations  14.3 us (8%)
  matrix products  10.8 us (6%)
  other arithmetic  3.95 us (2%)
    ppermute x10, starting transfers between devices, _allreduce_doubling(): lax.ppermute(flat, ('blk', 'rep'), [(i, i ^ mask) for i in range(total)])  50.8 us
    all_gather x1, waiting for transfers between devices, per_device(): gathered = lax.all_gather(features, 'blk', axis=0, tiled=True)  50.4 us
    ppermute x10, waiting for transfers between devices, _allreduce_doubling(): lax.ppermute(flat, ('blk', 'rep'), [(i, i ^ mask) for i in range(total)])  26 us
    ppermute x2, starting transfers between devices, _allreduce_doubling(): lax.ppermute(send, ('blk', 'rep'), [(i, i ^ mask) for i in range(total)])  4.11 us
    ppermute x2, waiting for transfers between devices, _allreduce_doubling(): lax.ppermute(send, ('blk', 'rep'), [(i, i ^ mask) for i in range(total)])  4.05 us
    dot_general x1, matrix products, per_device(): jnp.einsum('tcji,cjf->tif', selected, gathered, preferred_element_type=jn...  3.9 us
  transfers between devices with their start and end apart: 14, of which 13 were waited for; matrix products, arithmetic and copies ran while one was open for 8% of the time, Pallas kernels for 0%

profile of v4, /device:TPU:15, one launch (start us, length us, event | category | flops | bytes accessed | tf_op | source)
XLA Modules:
  0.0 166.9 jit_solution(16094962302575368895)
XLA Ops:
  13.3 3.3 %convolution_bitcast_fusion = f32[32,128,256]{2,1,0:T(8,128)} fusion(bf16[2,128,256,1]{2,1,0,3:T(8,128)(2,1)S(1)} %bitcast.36, bf16[2,32,128,128]{3,1,2,0:T(8,128)(2,1)S(1)} %convolution_convert_fusion), kind=kOutput, calls=%fused_computation | convolution fusion | flops 536870912 | bytes 6422528 | tf_op jit(solution)/shard_map/tcji,tif->cjf/dot_general | solution.py:43
  16.7 50.4 %all-gather.2.cloned.1.call-done = bf16[32,128,256]{2,1,0:T(8,128)(2,1)} async-done(((bf16[2,128,256]{2,1,0:T(8,128)(2,1)}), bf16[32,128,256]{2,1,0:T(8,128)(2,1)}) %all-gather.2.cloned.1.call-update) | async-done | bytes 2097168 | tf_op jit(solution)/shard_map/all_gather | solution.py:24
  67.1 3.9 %fusion.8 = bf16[2,128,256]{2,1,0:T(8,128)(2,1)S(1)} fusion(bf16[2,32,128,128]{3,1,2,0:T(8,128)(2,1)} %copy-done.1, bf16[32,128,256,1]{2,1,0,3:T(8,128)(2,1)} %bitcast.42), kind=kOutput, calls=%fused_computation.11 | convolution fusion | flops 536936448 | bytes 4325376 | tf_op jit(solution)/shard_map/tcji,cjf->tif/dot_general | solution.py:25
  71.4 2.2 %collective-permute-start = (f32[32768]{0:T(1024)S(1)}, f32[32768]{0:T(1024)S(1)}, u32[]{:S(2)}, u32[]{:S(2)}) collective-permute-start(f32[32768]{0:T(1024)S(1)} %bitcast.41), channel_id=1, source_target_pairs={{0,64},{1,65},{2,66},{3,67},{4,68},{5,69},{6,70},{7,71},{8,72},{9,... | collective-permute-start | bytes 393224 | tf_op jit(solution)/shard_map/ppermute | solution.py:71
  74.6 1.9 %collective-permute-start.1 = (f32[16384]{0:T(1024)S(1)}, f32[16384]{0:T(1024)S(1)}, u32[]{:S(2)}, u32[]{:S(2)}) collective-permute-start(f32[16384]{0:T(1024)S(1)} %slice_select_fusion), channel_id=1, source_target_pairs={{0,1},{1,0},{2,3},{3,2},{4,5},{5,4},{6,7},{7,6},{8,9},{9,8},{10,11... | collective-permute-start | bytes 196616 | tf_op jit(solution)/shard_map/ppermute | solution.py:71
  76.6 3.1 %collective-permute-done.1 = f32[16384]{0:T(1024)S(1)} collective-permute-done((f32[16384]{0:T(1024)S(1)}, f32[16384]{0:T(1024)S(1)}, u32[]{:S(2)}, u32[]{:S(2)}) %collective-permute-start.1) | collective-permute-done | bytes 65568 | tf_op jit(solution)/shard_map/ppermute | solution.py:71
  79.7 2.3 %collective-permute-start.2 = (f32[16384]{0:T(1024)S(1)}, f32[16384]{0:T(1024)S(1)}, u32[]{:S(2)}, u32[]{:S(2)}) collective-permute-start(f32[16384]{0:T(1024)S(1)} %select_add_fusion), channel_id=1, source_target_pairs={{0,8},{1,9},{2,10},{3,11},{4,12},{5,13},{6,14},{7,15},{8,0},{9,1},... | collective-permute-start | bytes 196616 | tf_op jit(solution)/shard_map/ppermute | solution.py:73
  82.0 2.8 %collective-permute-done.2 = f32[16384]{0:T(1024)S(1)} collective-permute-done((f32[16384]{0:T(1024)S(1)}, f32[16384]{0:T(1024)S(1)}, u32[]{:S(2)}, u32[]{:S(2)}) %collective-permute-start.2) | collective-permute-done | bytes 65568 | tf_op jit(solution)/shard_map/ppermute | solution.py:73
  84.8 1.9 %collective-permute-start.3 = (f32[16384]{0:T(1024)S(1)}, f32[16384]{0:T(1024)S(1)}, u32[]{:S(2)}, u32[]{:S(2)}) collective-permute-start(f32[16384]{0:T(1024)S(1)} %add.50), channel_id=1, source_target_pairs={{0,128},{1,129},{2,130},{3,131},{4,132},{5,133},{6,134},{7,135},{8... | collective-permute-start | bytes 196616 | tf_op jit(solution)/shard_map/ppermute | solution.py:73
  86.8 3.2 %collective-permute-done.3 = f32[16384]{0:T(1024)S(1)} collective-permute-done((f32[16384]{0:T(1024)S(1)}, f32[16384]{0:T(1024)S(1)}, u32[]{:S(2)}, u32[]{:S(2)}) %collective-permute-start.3) | collective-permute-done | bytes 65568 | tf_op jit(solution)/shard_map/ppermute | solution.py:73
  90.0 3.8 %collective-permute-start.4 = (f32[16384]{0:T(1024)S(1)}, f32[16384]{0:T(1024)S(1)}, u32[]{:S(2)}, u32[]{:S(2)}) collective-permute-start(f32[16384]{0:T(1024)S(1)} %add.51), channel_id=1, source_target_pairs={{0,2},{1,3},{2,0},{3,1},{4,6},{5,7},{6,4},{7,5},{8,10},{9,11},{10,... | collective-permute-start | bytes 196616 | tf_op jit(solution)/shard_map/ppermute | solution.py:73
  93.7 2.1 %collective-permute-done.4 = f32[16384]{0:T(1024)S(1)} collective-permute-done((f32[16384]{0:T(1024)S(1)}, f32[16384]{0:T(1024)S(1)}, u32[]{:S(2)}, u32[]{:S(2)}) %collective-permute-start.4) | collective-permute-done | bytes 65568 | tf_op jit(solution)/shard_map/ppermute | solution.py:73
  95.9 7.6 %collective-permute-start.5 = (f32[16384]{0:T(1024)S(1)}, f32[16384]{0:T(1024)S(1)}, u32[]{:S(2)}, u32[]{:S(2)}) collective-permute-start(f32[16384]{0:T(1024)S(1)} %add.52), channel_id=1, source_target_pairs={{0,4},{1,5},{2,6},{3,7},{4,0},{5,1},{6,2},{7,3},{8,12},{9,13},{10,... | collective-permute-start | bytes 196616 | tf_op jit(solution)/shard_map/ppermute | solution.py:73
  103.5 1.7 %collective-permute-done.5 = f32[16384]{0:T(1024)S(1)} collective-permute-done((f32[16384]{0:T(1024)S(1)}, f32[16384]{0:T(1024)S(1)}, u32[]{:S(2)}, u32[]{:S(2)}) %collective-permute-start.5) | collective-permute-done | bytes 65568 | tf_op jit(solution)/shard_map/ppermute | solution.py:73
  105.2 4.7 %collective-permute-start.6 = (f32[16384]{0:T(1024)S(1)}, f32[16384]{0:T(1024)S(1)}, u32[]{:S(2)}, u32[]{:S(2)}) collective-permute-start(f32[16384]{0:T(1024)S(1)} %add.53), channel_id=1, source_target_pairs={{0,16},{1,17},{2,18},{3,19},{4,20},{5,21},{6,22},{7,23},{8,24},{9,... | collective-permute-start | bytes 196616 | tf_op jit(solution)/shard_map/ppermute | solution.py:73
  111.6 8.7 %collective-permute-start.7 = (f32[16384]{0:T(1024)S(1)}, f32[16384]{0:T(1024)S(1)}, u32[]{:S(2)}, u32[]{:S(2)}) collective-permute-start(f32[16384]{0:T(1024)S(1)} %add.54), channel_id=1, source_target_pairs={{0,32},{1,33},{2,34},{3,35},{4,36},{5,37},{6,38},{7,39},{8,40},{9,... | collective-permute-start | bytes 196616 | tf_op jit(solution)/shard_map/ppermute | solution.py:73
  120.3 2.3 %collective-permute-done.7 = f32[16384]{0:T(1024)S(1)} collective-permute-done((f32[16384]{0:T(1024)S(1)}, f32[16384]{0:T(1024)S(1)}, u32[]{:S(2)}, u32[]{:S(2)}) %collective-permute-start.7) | collective-permute-done | bytes 65568 | tf_op jit(solution)/shard_map/ppermute | solution.py:73
  122.7 2.9 %collective-permute-start.8 = (f32[16384]{0:T(1024)S(1)}, f32[16384]{0:T(1024)S(1)}, u32[]{:S(2)}, u32[]{:S(2)}) collective-permute-start(f32[16384]{0:T(1024)S(1)} %add.55), channel_id=1, source_target_pairs={{0,256},{1,257},{2,258},{3,259},{4,260},{5,261},{6,262},{7,263},{8... | collective-permute-start | bytes 196616 | tf_op jit(solution)/shard_map/ppermute | solution.py:73
  125.6 4.1 %collective-permute-done.8 = f32[16384]{0:T(1024)S(1)} collective-permute-done((f32[16384]{0:T(1024)S(1)}, f32[16384]{0:T(1024)S(1)}, u32[]{:S(2)}, u32[]{:S(2)}) %collective-permute-start.8) | collective-permute-done | bytes 65568 | tf_op jit(solution)/shard_map/ppermute | solution.py:73
  129.7 4.3 %collective-permute-start.9 = (f32[16384]{0:T(1024)S(1)}, f32[16384]{0:T(1024)S(1)}, u32[]{:S(2)}, u32[]{:S(2)}) collective-permute-start(f32[16384]{0:T(1024)S(1)} %add.56), channel_id=1, source_target_pairs={{0,512},{1,513},{2,514},{3,515},{4,516},{5,517},{6,518},{7,519},{8... | collective-permute-start | bytes 196616 | tf_op jit(solution)/shard_map/ppermute | solution.py:73
  134.0 5.2 %collective-permute-done.9 = f32[16384]{0:T(1024)S(1)} collective-permute-done((f32[16384]{0:T(1024)S(1)}, f32[16384]{0:T(1024)S(1)}, u32[]{:S(2)}, u32[]{:S(2)}) %collective-permute-start.9) | collective-permute-done | bytes 65568 | tf_op jit(solution)/shard_map/ppermute | solution.py:73
  139.2 2.3 %collective-permute-start.10 = (f32[16384]{0:T(1024)S(1)}, f32[16384]{0:T(1024)S(1)}, u32[]{:S(2)}, u32[]{:S(2)}) collective-permute-start(f32[16384]{0:T(1024)S(1)} %add.57), channel_id=1, source_target_pairs={{0,1},{1,0},{2,3},{3,2},{4,5},{5,4},{6,7},{7,6},{8,9},{9,8},{10,11... | collective-permute-start | bytes 196616 | tf_op jit(solution)/shard_map/ppermute | solution.py:76
  141.5 2.7 %collective-permute-done.10 = f32[16384]{0:T(1024)S(1)} collective-permute-done((f32[16384]{0:T(1024)S(1)}, f32[16384]{0:T(1024)S(1)}, u32[]{:S(2)}, u32[]{:S(2)}) %collective-permute-start.10) | collective-permute-done | bytes 65568 | tf_op jit(solution)/shard_map/ppermute | solution.py:76
  144.3 12.4 %collective-permute-start.11 = (f32[32768]{0:T(1024)S(1)}, f32[32768]{0:T(1024)S(1)}, u32[]{:S(2)}, u32[]{:S(2)}) collective-permute-start(f32[32768]{0:T(1024)S(1)} %pad_maximum_fusion), channel_id=1, source_target_pairs={{0,64},{1,65},{2,66},{3,67},{4,68},{5,69},{6,70},{7,71},{8,72},{9,... | collective-permute-start | bytes 393224 | tf_op jit(solution)/shard_map/ppermute | solution.py:76
  (45 shorter events, 12.7 us)
Async XLA Ops:
  7.2 3.4 %copy-start = (bf16[2,24,128,128]{3,2,1,0:T(8,128)(2,1)S(1)}, bf16[2,24,128,128]{3,2,1,0:T(8,128)(2,1)}, u32[]{:S(2)}) copy-start(bf16[2,24,128,128]{3,2,1,0:T(8,128)(2,1)} %param.9) | copy-start | bytes 4718596
  7.2 59.9 %all-gather.2.cloned.1.call-start = ((), (), s32[]{:S(2)}) async-start(), calls=%async_computation.1 | async-start | bytes 2228224 | tf_op jit(solution)/shard_map/all_gather | solution.py:24
  7.9 150.5 %reduce-scatter.2.cloned.1.call-start = ((), (), s32[]{:S(2)}) async-start(), calls=%async_computation.2 | async-start | bytes 4456448 | tf_op jit(solution)/shard_map/reduce_scatter | solution.py:42
  12.0 1.4 copy-start.1
  67.1 3.9 %copy-start.3 = (bf16[2,128,256]{2,1,0:T(8,128)(2,1)S(1)}, bf16[2,128,256]{2,1,0:T(8,128)(2,1)}, u32[]{:S(2)}) copy-start(bf16[2,128,256]{2,1,0:T(8,128)(2,1)} %param.12) | copy-start | bytes 393220
  71.3 85.4 %copy-start.2 = (bf16[256,256]{1,0:T(8,128)(2,1)S(1)}, bf16[256,256]{1,0:T(8,128)(2,1)}, u32[]{:S(2)}) copy-start(bf16[256,256]{1,0:T(8,128)(2,1)} %param.8) | copy-start | bytes 393220
  71.4 3.2 %collective-permute-start = (f32[32768]{0:T(1024)S(1)}, f32[32768]{0:T(1024)S(1)}, u32[]{:S(2)}, u32[]{:S(2)}) collective-permute-start(f32[32768]{0:T(1024)S(1)} %bitcast.41), channel_id=1, source_target_pairs={{0,64},{1,65},{2,66},{3,67},{4,68},{5,69},{6,70},{7,71},{8,72},{9,... | collective-permute-start | bytes 393224 | tf_op jit(solution)/shard_map/ppermute | solution.py:71
  74.6 5.0 %collective-permute-start.1 = (f32[16384]{0:T(1024)S(1)}, f32[16384]{0:T(1024)S(1)}, u32[]{:S(2)}, u32[]{:S(2)}) collective-permute-start(f32[16384]{0:T(1024)S(1)} %slice_select_fusion), channel_id=1, source_target_pairs={{0,1},{1,0},{2,3},{3,2},{4,5},{5,4},{6,7},{7,6},{8,9},{9,8},{10,11... | collective-permute-start | bytes 196616 | tf_op jit(solution)/shard_map/ppermute | solution.py:71
  79.7 78.8 %copy-start.4 = (s32[2,128,256]{2,1,0:T(8,128)S(1)}, s32[2,128,256]{2,1,0:T(8,128)}, u32[]{:S(2)}) copy-start(s32[2,128,256]{2,1,0:T(8,128)} %param.13) | copy-start | bytes 786436
  79.7 5.1 %collective-permute-start.2 = (f32[16384]{0:T(1024)S(1)}, f32[16384]{0:T(1024)S(1)}, u32[]{:S(2)}, u32[]{:S(2)}) collective-permute-start(f32[16384]{0:T(1024)S(1)} %select_add_fusion), channel_id=1, source_target_pairs={{0,8},{1,9},{2,10},{3,11},{4,12},{5,13},{6,14},{7,15},{8,0},{9,1},... | collective-permute-start | bytes 196616 | tf_op jit(solution)/shard_map/ppermute | solution.py:73
  84.8 5.1 %collective-permute-start.3 = (f32[16384]{0:T(1024)S(1)}, f32[16384]{0:T(1024)S(1)}, u32[]{:S(2)}, u32[]{:S(2)}) collective-permute-start(f32[16384]{0:T(1024)S(1)} %add.50), channel_id=1, source_target_pairs={{0,128},{1,129},{2,130},{3,131},{4,132},{5,133},{6,134},{7,135},{8... | collective-permute-start | bytes 196616 | tf_op jit(solution)/shard_map/ppermute | solution.py:73
  90.0 5.9 %collective-permute-start.4 = (f32[16384]{0:T(1024)S(1)}, f32[16384]{0:T(1024)S(1)}, u32[]{:S(2)}, u32[]{:S(2)}) collective-permute-start(f32[16384]{0:T(1024)S(1)} %add.51), channel_id=1, source_target_pairs={{0,2},{1,3},{2,0},{3,1},{4,6},{5,7},{6,4},{7,5},{8,10},{9,11},{10,... | collective-permute-start | bytes 196616 | tf_op jit(solution)/shard_map/ppermute | solution.py:73
  95.9 9.3 %collective-permute-start.5 = (f32[16384]{0:T(1024)S(1)}, f32[16384]{0:T(1024)S(1)}, u32[]{:S(2)}, u32[]{:S(2)}) collective-permute-start(f32[16384]{0:T(1024)S(1)} %add.52), channel_id=1, source_target_pairs={{0,4},{1,5},{2,6},{3,7},{4,0},{5,1},{6,2},{7,3},{8,12},{9,13},{10,... | collective-permute-start | bytes 196616 | tf_op jit(solution)/shard_map/ppermute | solution.py:73
  105.2 6.4 %collective-permute-start.6 = (f32[16384]{0:T(1024)S(1)}, f32[16384]{0:T(1024)S(1)}, u32[]{:S(2)}, u32[]{:S(2)}) collective-permute-start(f32[16384]{0:T(1024)S(1)} %add.53), channel_id=1, source_target_pairs={{0,16},{1,17},{2,18},{3,19},{4,20},{5,21},{6,22},{7,23},{8,24},{9,... | collective-permute-start | bytes 196616 | tf_op jit(solution)/shard_map/ppermute | solution.py:73
  111.6 11.0 %collective-permute-start.7 = (f32[16384]{0:T(1024)S(1)}, f32[16384]{0:T(1024)S(1)}, u32[]{:S(2)}, u32[]{:S(2)}) collective-permute-start(f32[16384]{0:T(1024)S(1)} %add.54), channel_id=1, source_target_pairs={{0,32},{1,33},{2,34},{3,35},{4,36},{5,37},{6,38},{7,39},{8,40},{9,... | collective-permute-start | bytes 196616 | tf_op jit(solution)/shard_map/ppermute | solution.py:73
  122.7 7.0 %collective-permute-start.8 = (f32[16384]{0:T(1024)S(1)}, f32[16384]{0:T(1024)S(1)}, u32[]{:S(2)}, u32[]{:S(2)}) collective-permute-start(f32[16384]{0:T(1024)S(1)} %add.55), channel_id=1, source_target_pairs={{0,256},{1,257},{2,258},{3,259},{4,260},{5,261},{6,262},{7,263},{8... | collective-permute-start | bytes 196616 | tf_op jit(solution)/shard_map/ppermute | solution.py:73
  129.7 9.5 %collective-permute-start.9 = (f32[16384]{0:T(1024)S(1)}, f32[16384]{0:T(1024)S(1)}, u32[]{:S(2)}, u32[]{:S(2)}) collective-permute-start(f32[16384]{0:T(1024)S(1)} %add.56), channel_id=1, source_target_pairs={{0,512},{1,513},{2,514},{3,515},{4,516},{5,517},{6,518},{7,519},{8... | collective-permute-start | bytes 196616 | tf_op jit(solution)/shard_map/ppermute | solution.py:73
  139.2 5.0 %collective-permute-start.10 = (f32[16384]{0:T(1024)S(1)}, f32[16384]{0:T(1024)S(1)}, u32[]{:S(2)}, u32[]{:S(2)}) collective-permute-start(f32[16384]{0:T(1024)S(1)} %add.57), channel_id=1, source_target_pairs={{0,1},{1,0},{2,3},{3,2},{4,5},{5,4},{6,7},{7,6},{8,9},{9,8},{10,11... | collective-permute-start | bytes 196616 | tf_op jit(solution)/shard_map/ppermute | solution.py:76
  144.3 13.4 %collective-permute-start.11 = (f32[32768]{0:T(1024)S(1)}, f32[32768]{0:T(1024)S(1)}, u32[]{:S(2)}, u32[]{:S(2)}) collective-permute-start(f32[32768]{0:T(1024)S(1)} %pad_maximum_fusion), channel_id=1, source_target_pairs={{0,64},{1,65},{2,66},{3,67},{4,68},{5,69},{6,70},{7,71},{8,72},{9,... | collective-permute-start | bytes 393224 | tf_op jit(solution)/shard_map/ppermute | solution.py:76
Sparse Core Ops, SparseCore 0:
  10.7 56.3 all-gather.1
  70.5 67.9 reduce-scatter.1

commit v5 on v4

--- a/solution.py
+++ b/solution.py
@@ -40,7 +40,7 @@
     )
     row_grad = row_grad.astype(jnp.bfloat16).reshape(out_grad.shape)
     spread = lax.psum_scatter(
-        jnp.einsum("tcji,tif->cjf", selected, row_grad, preferred_element_type=jnp.float32),
+        jnp.einsum("tcji,tif->cjf", selected, row_grad, preferred_element_type=jnp.float32).astype(jnp.bfloat16),
         "blk",
         scatter_dimension=0,
         tiled=True,

time: 169 us -> 168 us (level)
  transfers between devices with their start and end apart: 14 -> 14, of which waited for: 13 -> 12; matrix products, arithmetic and copies ran while one was open for 8% -> 8% of each run, Pallas kernels for 0% -> 0%
where the time goes in v5:
time: 168 us; the launch traced here: 166 us
  waiting for transfers between devices  80.6 us (48%)
  starting transfers between devices  55.4 us (33%)
  between operations  14.4 us (9%)
  matrix products  10.3 us (6%)
  other arithmetic  3.91 us (2%)
    ppermute x10, starting transfers between devices, _allreduce_doubling(): lax.ppermute(flat, ('blk', 'rep'), [(i, i ^ mask) for i in range(total)])  51.2 us
    all_gather x1, waiting for transfers between devices, per_device(): gathered = lax.all_gather(features, 'blk', axis=0, tiled=True)  51.1 us
    ppermute x10, waiting for transfers between devices, _allreduce_doubling(): lax.ppermute(flat, ('blk', 'rep'), [(i, i ^ mask) for i in range(total)])  24.7 us
    ppermute x2, starting transfers between devices, _allreduce_doubling(): lax.ppermute(send, ('blk', 'rep'), [(i, i ^ mask) for i in range(total)])  4.11 us
    ppermute x2, waiting for transfers between devices, _allreduce_doubling(): lax.ppermute(send, ('blk', 'rep'), [(i, i ^ mask) for i in range(total)])  4.05 us
    dot_general x1, matrix products, per_device(): jnp.einsum('tcji,cjf->tif', selected, gathered, preferred_element_type=jn...  3.9 us
  transfers between devices with their start and end apart: 14, of which 12 were waited for; matrix products, arithmetic and copies ran while one was open for 8% of the time, Pallas kernels for 0%

profile of v5, /device:TPU:15, one launch (start us, length us, event | category | flops | bytes accessed | tf_op | source)
XLA Modules:
  0.0 166.0 jit_solution(14547524031948144008)
XLA Ops:
  13.3 2.7 %bitcast_convert_fusion = bf16[32,128,256]{2,1,0:T(8,128)(2,1)} fusion(bf16[2,128,256,1]{2,1,0,3:T(8,128)(2,1)S(1)} %bitcast.36, bf16[2,32,128,128]{3,1,2,0:T(8,128)(2,1)S(1)} %convolution_convert_fusion), kind=kOutput, calls=%fused_computation | convolution fusion | flops 537919488 | bytes 4325376 | tf_op jit(solution)/shard_map/tcji,tif->cjf/dot_general | solution.py:43
  16.0 51.1 %all-gather.2.cloned.1.call-done = bf16[32,128,256]{2,1,0:T(8,128)(2,1)} async-done(((bf16[2,128,256]{2,1,0:T(8,128)(2,1)}), bf16[32,128,256]{2,1,0:T(8,128)(2,1)}) %all-gather.2.cloned.1.call-update) | async-done | bytes 2097168 | tf_op jit(solution)/shard_map/all_gather | solution.py:24
  67.1 3.9 %fusion.8 = bf16[2,128,256]{2,1,0:T(8,128)(2,1)S(1)} fusion(bf16[2,32,128,128]{3,1,2,0:T(8,128)(2,1)} %copy-done.1, bf16[32,128,256,1]{2,1,0,3:T(8,128)(2,1)} %bitcast.42), kind=kOutput, calls=%fused_computation.11 | convolution fusion | flops 536936448 | bytes 4325376 | tf_op jit(solution)/shard_map/tcji,cjf->tif/dot_general | solution.py:25
  71.4 2.2 %collective-permute-start = (f32[32768]{0:T(1024)S(1)}, f32[32768]{0:T(1024)S(1)}, u32[]{:S(2)}, u32[]{:S(2)}) collective-permute-start(f32[32768]{0:T(1024)S(1)} %bitcast.41), channel_id=1, source_target_pairs={{0,64},{1,65},{2,66},{3,67},{4,68},{5,69},{6,70},{7,71},{8,72},{9,... | collective-permute-start | bytes 393224 | tf_op jit(solution)/shard_map/ppermute | solution.py:71
  74.7 1.9 %collective-permute-start.1 = (f32[16384]{0:T(1024)S(1)}, f32[16384]{0:T(1024)S(1)}, u32[]{:S(2)}, u32[]{:S(2)}) collective-permute-start(f32[16384]{0:T(1024)S(1)} %slice_select_fusion), channel_id=1, source_target_pairs={{0,1},{1,0},{2,3},{3,2},{4,5},{5,4},{6,7},{7,6},{8,9},{9,8},{10,11... | collective-permute-start | bytes 196616 | tf_op jit(solution)/shard_map/ppermute | solution.py:71
  76.6 3.1 %collective-permute-done.1 = f32[16384]{0:T(1024)S(1)} collective-permute-done((f32[16384]{0:T(1024)S(1)}, f32[16384]{0:T(1024)S(1)}, u32[]{:S(2)}, u32[]{:S(2)}) %collective-permute-start.1) | collective-permute-done | bytes 65568 | tf_op jit(solution)/shard_map/ppermute | solution.py:71
  79.7 2.1 %collective-permute-start.2 = (f32[16384]{0:T(1024)S(1)}, f32[16384]{0:T(1024)S(1)}, u32[]{:S(2)}, u32[]{:S(2)}) collective-permute-start(f32[16384]{0:T(1024)S(1)} %select_add_fusion), channel_id=1, source_target_pairs={{0,8},{1,9},{2,10},{3,11},{4,12},{5,13},{6,14},{7,15},{8,0},{9,1},... | collective-permute-start | bytes 196616 | tf_op jit(solution)/shard_map/ppermute | solution.py:73
  81.8 2.9 %collective-permute-done.2 = f32[16384]{0:T(1024)S(1)} collective-permute-done((f32[16384]{0:T(1024)S(1)}, f32[16384]{0:T(1024)S(1)}, u32[]{:S(2)}, u32[]{:S(2)}) %collective-permute-start.2) | collective-permute-done | bytes 65568 | tf_op jit(solution)/shard_map/ppermute | solution.py:73
  84.7 1.9 %collective-permute-start.3 = (f32[16384]{0:T(1024)S(1)}, f32[16384]{0:T(1024)S(1)}, u32[]{:S(2)}, u32[]{:S(2)}) collective-permute-start(f32[16384]{0:T(1024)S(1)} %add.50), channel_id=1, source_target_pairs={{0,128},{1,129},{2,130},{3,131},{4,132},{5,133},{6,134},{7,135},{8... | collective-permute-start | bytes 196616 | tf_op jit(solution)/shard_map/ppermute | solution.py:73
  86.6 3.1 %collective-permute-done.3 = f32[16384]{0:T(1024)S(1)} collective-permute-done((f32[16384]{0:T(1024)S(1)}, f32[16384]{0:T(1024)S(1)}, u32[]{:S(2)}, u32[]{:S(2)}) %collective-permute-start.3) | collective-permute-done | bytes 65568 | tf_op jit(solution)/shard_map/ppermute | solution.py:73
  89.7 4.0 %collective-permute-start.4 = (f32[16384]{0:T(1024)S(1)}, f32[16384]{0:T(1024)S(1)}, u32[]{:S(2)}, u32[]{:S(2)}) collective-permute-start(f32[16384]{0:T(1024)S(1)} %add.51), channel_id=1, source_target_pairs={{0,2},{1,3},{2,0},{3,1},{4,6},{5,7},{6,4},{7,5},{8,10},{9,11},{10,... | collective-permute-start | bytes 196616 | tf_op jit(solution)/shard_map/ppermute | solution.py:73
  93.7 1.9 %collective-permute-done.4 = f32[16384]{0:T(1024)S(1)} collective-permute-done((f32[16384]{0:T(1024)S(1)}, f32[16384]{0:T(1024)S(1)}, u32[]{:S(2)}, u32[]{:S(2)}) %collective-permute-start.4) | collective-permute-done | bytes 65568 | tf_op jit(solution)/shard_map/ppermute | solution.py:73
  95.7 7.8 %collective-permute-start.5 = (f32[16384]{0:T(1024)S(1)}, f32[16384]{0:T(1024)S(1)}, u32[]{:S(2)}, u32[]{:S(2)}) collective-permute-start(f32[16384]{0:T(1024)S(1)} %add.52), channel_id=1, source_target_pairs={{0,4},{1,5},{2,6},{3,7},{4,0},{5,1},{6,2},{7,3},{8,12},{9,13},{10,... | collective-permute-start | bytes 196616 | tf_op jit(solution)/shard_map/ppermute | solution.py:73
  103.4 1.7 %collective-permute-done.5 = f32[16384]{0:T(1024)S(1)} collective-permute-done((f32[16384]{0:T(1024)S(1)}, f32[16384]{0:T(1024)S(1)}, u32[]{:S(2)}, u32[]{:S(2)}) %collective-permute-start.5) | collective-permute-done | bytes 65568 | tf_op jit(solution)/shard_map/ppermute | solution.py:73
  105.2 4.7 %collective-permute-start.6 = (f32[16384]{0:T(1024)S(1)}, f32[16384]{0:T(1024)S(1)}, u32[]{:S(2)}, u32[]{:S(2)}) collective-permute-start(f32[16384]{0:T(1024)S(1)} %add.53), channel_id=1, source_target_pairs={{0,16},{1,17},{2,18},{3,19},{4,20},{5,21},{6,22},{7,23},{8,24},{9,... | collective-permute-start | bytes 196616 | tf_op jit(solution)/shard_map/ppermute | solution.py:73
  109.9 1.6 collective-permute-done.6
  111.6 8.5 %collective-permute-start.7 = (f32[16384]{0:T(1024)S(1)}, f32[16384]{0:T(1024)S(1)}, u32[]{:S(2)}, u32[]{:S(2)}) collective-permute-start(f32[16384]{0:T(1024)S(1)} %add.54), channel_id=1, source_target_pairs={{0,32},{1,33},{2,34},{3,35},{4,36},{5,37},{6,38},{7,39},{8,40},{9,... | collective-permute-start | bytes 196616 | tf_op jit(solution)/shard_map/ppermute | solution.py:73
  120.1 2.4 %collective-permute-done.7 = f32[16384]{0:T(1024)S(1)} collective-permute-done((f32[16384]{0:T(1024)S(1)}, f32[16384]{0:T(1024)S(1)}, u32[]{:S(2)}, u32[]{:S(2)}) %collective-permute-start.7) | collective-permute-done | bytes 65568 | tf_op jit(solution)/shard_map/ppermute | solution.py:73
  122.5 2.7 %collective-permute-start.8 = (f32[16384]{0:T(1024)S(1)}, f32[16384]{0:T(1024)S(1)}, u32[]{:S(2)}, u32[]{:S(2)}) collective-permute-start(f32[16384]{0:T(1024)S(1)} %add.55), channel_id=1, source_target_pairs={{0,256},{1,257},{2,258},{3,259},{4,260},{5,261},{6,262},{7,263},{8... | collective-permute-start | bytes 196616 | tf_op jit(solution)/shard_map/ppermute | solution.py:73
  125.2 3.8 %collective-permute-done.8 = f32[16384]{0:T(1024)S(1)} collective-permute-done((f32[16384]{0:T(1024)S(1)}, f32[16384]{0:T(1024)S(1)}, u32[]{:S(2)}, u32[]{:S(2)}) %collective-permute-start.8) | collective-permute-done | bytes 65568 | tf_op jit(solution)/shard_map/ppermute | solution.py:73
  129.0 3.3 %collective-permute-start.9 = (f32[16384]{0:T(1024)S(1)}, f32[16384]{0:T(1024)S(1)}, u32[]{:S(2)}, u32[]{:S(2)}) collective-permute-start(f32[16384]{0:T(1024)S(1)} %add.56), channel_id=1, source_target_pairs={{0,512},{1,513},{2,514},{3,515},{4,516},{5,517},{6,518},{7,519},{8... | collective-permute-start | bytes 196616 | tf_op jit(solution)/shard_map/ppermute | solution.py:73
  132.3 6.1 %collective-permute-done.9 = f32[16384]{0:T(1024)S(1)} collective-permute-done((f32[16384]{0:T(1024)S(1)}, f32[16384]{0:T(1024)S(1)}, u32[]{:S(2)}, u32[]{:S(2)}) %collective-permute-start.9) | collective-permute-done | bytes 65568 | tf_op jit(solution)/shard_map/ppermute | solution.py:73
  138.4 2.9 %collective-permute-start.10 = (f32[16384]{0:T(1024)S(1)}, f32[16384]{0:T(1024)S(1)}, u32[]{:S(2)}, u32[]{:S(2)}) collective-permute-start(f32[16384]{0:T(1024)S(1)} %add.57), channel_id=1, source_target_pairs={{0,1},{1,0},{2,3},{3,2},{4,5},{5,4},{6,7},{7,6},{8,9},{9,8},{10,11... | collective-permute-start | bytes 196616 | tf_op jit(solution)/shard_map/ppermute | solution.py:76
  143.5 13.2 %collective-permute-start.11 = (f32[32768]{0:T(1024)S(1)}, f32[32768]{0:T(1024)S(1)}, u32[]{:S(2)}, u32[]{:S(2)}) collective-permute-start(f32[32768]{0:T(1024)S(1)} %pad_maximum_fusion), channel_id=1, source_target_pairs={{0,64},{1,65},{2,66},{3,67},{4,68},{5,69},{6,70},{7,71},{8,72},{9,... | collective-permute-start | bytes 393224 | tf_op jit(solution)/shard_map/ppermute | solution.py:76
  (45 shorter events, 12.1 us)
Async XLA Ops:
  7.2 3.4 %copy-start = (bf16[2,24,128,128]{3,2,1,0:T(8,128)(2,1)S(1)}, bf16[2,24,128,128]{3,2,1,0:T(8,128)(2,1)}, u32[]{:S(2)}) copy-start(bf16[2,24,128,128]{3,2,1,0:T(8,128)(2,1)} %param.9) | copy-start | bytes 4718596
  7.2 59.9 %all-gather.2.cloned.1.call-start = ((), (), s32[]{:S(2)}) async-start(), calls=%async_computation.1 | async-start | bytes 2228224 | tf_op jit(solution)/shard_map/all_gather | solution.py:24
  7.9 148.8 %reduce-scatter.2.cloned.1.call-start = ((), (), s32[]{:S(2)}) async-start(), calls=%async_computation.2 | async-start | bytes 2228224 | tf_op jit(solution)/shard_map/reduce_scatter | solution.py:42
  12.0 1.3 copy-start.1
  67.1 3.9 %copy-start.3 = (bf16[2,128,256]{2,1,0:T(8,128)(2,1)S(1)}, bf16[2,128,256]{2,1,0:T(8,128)(2,1)}, u32[]{:S(2)}) copy-start(bf16[2,128,256]{2,1,0:T(8,128)(2,1)} %param.12) | copy-start | bytes 393220
  71.0 70.3 %copy-start.2 = (bf16[256,256]{1,0:T(8,128)(2,1)S(1)}, bf16[256,256]{1,0:T(8,128)(2,1)}, u32[]{:S(2)}) copy-start(bf16[256,256]{1,0:T(8,128)(2,1)} %param.8) | copy-start | bytes 393220
  71.3 85.5 %copy-start.4 = (s32[2,128,256]{2,1,0:T(8,128)S(1)}, s32[2,128,256]{2,1,0:T(8,128)}, u32[]{:S(2)}) copy-start(s32[2,128,256]{2,1,0:T(8,128)} %param.13) | copy-start | bytes 786436
  71.4 3.2 %collective-permute-start = (f32[32768]{0:T(1024)S(1)}, f32[32768]{0:T(1024)S(1)}, u32[]{:S(2)}, u32[]{:S(2)}) collective-permute-start(f32[32768]{0:T(1024)S(1)} %bitcast.41), channel_id=1, source_target_pairs={{0,64},{1,65},{2,66},{3,67},{4,68},{5,69},{6,70},{7,71},{8,72},{9,... | collective-permute-start | bytes 393224 | tf_op jit(solution)/shard_map/ppermute | solution.py:71
  74.7 5.0 %collective-permute-start.1 = (f32[16384]{0:T(1024)S(1)}, f32[16384]{0:T(1024)S(1)}, u32[]{:S(2)}, u32[]{:S(2)}) collective-permute-start(f32[16384]{0:T(1024)S(1)} %slice_select_fusion), channel_id=1, source_target_pairs={{0,1},{1,0},{2,3},{3,2},{4,5},{5,4},{6,7},{7,6},{8,9},{9,8},{10,11... | collective-permute-start | bytes 196616 | tf_op jit(solution)/shard_map/ppermute | solution.py:71
  79.7 5.0 %collective-permute-start.2 = (f32[16384]{0:T(1024)S(1)}, f32[16384]{0:T(1024)S(1)}, u32[]{:S(2)}, u32[]{:S(2)}) collective-permute-start(f32[16384]{0:T(1024)S(1)} %select_add_fusion), channel_id=1, source_target_pairs={{0,8},{1,9},{2,10},{3,11},{4,12},{5,13},{6,14},{7,15},{8,0},{9,1},... | collective-permute-start | bytes 196616 | tf_op jit(solution)/shard_map/ppermute | solution.py:73
  84.7 5.0 %collective-permute-start.3 = (f32[16384]{0:T(1024)S(1)}, f32[16384]{0:T(1024)S(1)}, u32[]{:S(2)}, u32[]{:S(2)}) collective-permute-start(f32[16384]{0:T(1024)S(1)} %add.50), channel_id=1, source_target_pairs={{0,128},{1,129},{2,130},{3,131},{4,132},{5,133},{6,134},{7,135},{8... | collective-permute-start | bytes 196616 | tf_op jit(solution)/shard_map/ppermute | solution.py:73
  89.7 5.9 %collective-permute-start.4 = (f32[16384]{0:T(1024)S(1)}, f32[16384]{0:T(1024)S(1)}, u32[]{:S(2)}, u32[]{:S(2)}) collective-permute-start(f32[16384]{0:T(1024)S(1)} %add.51), channel_id=1, source_target_pairs={{0,2},{1,3},{2,0},{3,1},{4,6},{5,7},{6,4},{7,5},{8,10},{9,11},{10,... | collective-permute-start | bytes 196616 | tf_op jit(solution)/shard_map/ppermute | solution.py:73
  95.7 9.5 %collective-permute-start.5 = (f32[16384]{0:T(1024)S(1)}, f32[16384]{0:T(1024)S(1)}, u32[]{:S(2)}, u32[]{:S(2)}) collective-permute-start(f32[16384]{0:T(1024)S(1)} %add.52), channel_id=1, source_target_pairs={{0,4},{1,5},{2,6},{3,7},{4,0},{5,1},{6,2},{7,3},{8,12},{9,13},{10,... | collective-permute-start | bytes 196616 | tf_op jit(solution)/shard_map/ppermute | solution.py:73
  105.2 6.4 %collective-permute-start.6 = (f32[16384]{0:T(1024)S(1)}, f32[16384]{0:T(1024)S(1)}, u32[]{:S(2)}, u32[]{:S(2)}) collective-permute-start(f32[16384]{0:T(1024)S(1)} %add.53), channel_id=1, source_target_pairs={{0,16},{1,17},{2,18},{3,19},{4,20},{5,21},{6,22},{7,23},{8,24},{9,... | collective-permute-start | bytes 196616 | tf_op jit(solution)/shard_map/ppermute | solution.py:73
  111.6 10.9 %collective-permute-start.7 = (f32[16384]{0:T(1024)S(1)}, f32[16384]{0:T(1024)S(1)}, u32[]{:S(2)}, u32[]{:S(2)}) collective-permute-start(f32[16384]{0:T(1024)S(1)} %add.54), channel_id=1, source_target_pairs={{0,32},{1,33},{2,34},{3,35},{4,36},{5,37},{6,38},{7,39},{8,40},{9,... | collective-permute-start | bytes 196616 | tf_op jit(solution)/shard_map/ppermute | solution.py:73
  122.5 6.5 %collective-permute-start.8 = (f32[16384]{0:T(1024)S(1)}, f32[16384]{0:T(1024)S(1)}, u32[]{:S(2)}, u32[]{:S(2)}) collective-permute-start(f32[16384]{0:T(1024)S(1)} %add.55), channel_id=1, source_target_pairs={{0,256},{1,257},{2,258},{3,259},{4,260},{5,261},{6,262},{7,263},{8... | collective-permute-start | bytes 196616 | tf_op jit(solution)/shard_map/ppermute | solution.py:73
  129.0 9.4 %collective-permute-start.9 = (f32[16384]{0:T(1024)S(1)}, f32[16384]{0:T(1024)S(1)}, u32[]{:S(2)}, u32[]{:S(2)}) collective-permute-start(f32[16384]{0:T(1024)S(1)} %add.56), channel_id=1, source_target_pairs={{0,512},{1,513},{2,514},{3,515},{4,516},{5,517},{6,518},{7,519},{8... | collective-permute-start | bytes 196616 | tf_op jit(solution)/shard_map/ppermute | solution.py:73
  138.4 5.0 %collective-permute-start.10 = (f32[16384]{0:T(1024)S(1)}, f32[16384]{0:T(1024)S(1)}, u32[]{:S(2)}, u32[]{:S(2)}) collective-permute-start(f32[16384]{0:T(1024)S(1)} %add.57), channel_id=1, source_target_pairs={{0,1},{1,0},{2,3},{3,2},{4,5},{5,4},{6,7},{7,6},{8,9},{9,8},{10,11... | collective-permute-start | bytes 196616 | tf_op jit(solution)/shard_map/ppermute | solution.py:76
  143.5 14.9 %collective-permute-start.11 = (f32[32768]{0:T(1024)S(1)}, f32[32768]{0:T(1024)S(1)}, u32[]{:S(2)}, u32[]{:S(2)}) collective-permute-start(f32[32768]{0:T(1024)S(1)} %pad_maximum_fusion), channel_id=1, source_target_pairs={{0,64},{1,65},{2,66},{3,67},{4,68},{5,69},{6,70},{7,71},{8,72},{9,... | collective-permute-start | bytes 393224 | tf_op jit(solution)/shard_map/ppermute | solution.py:76
Sparse Core Ops, SparseCore 0:
  10.7 56.3 all-gather.1
  70.5 63.8 reduce-scatter.1

commit v6 on v4

--- a/solution.py
+++ b/solution.py
@@ -34,7 +34,7 @@
         hidden_flat, grad_flat, (((0,), (0,)), ((), ())), preferred_element_type=jnp.float32
     )
     node_count = row_tiles * blk_size * rep_size * tile_size
-    weight_grad = _allreduce_doubling(grad_term, blk_size, rep_size) * (1.0 / math.sqrt(node_count))
+    weight_grad = _allreduce_doubling(grad_term * (1.0 / math.sqrt(node_count)), blk_size, rep_size)
     row_grad = lax.dot_general(
         grad_flat, weight, (((1,), (1,)), ((), ())), preferred_element_type=jnp.float32
     )

time: 169 us -> 169 us (level)
  no operation moved by 1% of the time
where the time goes in v6:
time: 169 us; the launch traced here: 167 us
  waiting for transfers between devices  81.2 us (48%)
  starting transfers between devices  55 us (33%)
  between operations  14.3 us (8%)
  matrix products  10.8 us (6%)
  other arithmetic  3.95 us (2%)
    ppermute x10, starting transfers between devices, _allreduce_doubling(): lax.ppermute(flat, ('blk', 'rep'), [(i, i ^ mask) for i in range(total)])  50.8 us
    all_gather x1, waiting for transfers between devices, per_device(): gathered = lax.all_gather(features, 'blk', axis=0, tiled=True)  50.4 us
    ppermute x10, waiting for transfers between devices, _allreduce_doubling(): lax.ppermute(flat, ('blk', 'rep'), [(i, i ^ mask) for i in range(total)])  26 us
    ppermute x2, starting transfers between devices, _allreduce_doubling(): lax.ppermute(send, ('blk', 'rep'), [(i, i ^ mask) for i in range(total)])  4.11 us
    ppermute x2, waiting for transfers between devices, _allreduce_doubling(): lax.ppermute(send, ('blk', 'rep'), [(i, i ^ mask) for i in range(total)])  4.05 us
    dot_general x1, matrix products, per_device(): jnp.einsum('tcji,cjf->tif', selected, gathered, preferred_element_type=jn...  3.9 us
  transfers between devices with their start and end apart: 14, of which 13 were waited for; matrix products, arithmetic and copies ran while one was open for 8% of the time, Pallas kernels for 0%

profile of v6, /device:TPU:15, one launch (start us, length us, event | category | flops | bytes accessed | tf_op | source)
XLA Modules:
  0.0 166.9 jit_solution(9475591194869940231)
XLA Ops:
  13.3 3.3 %convolution_bitcast_fusion = f32[32,128,256]{2,1,0:T(8,128)} fusion(bf16[2,128,256,1]{2,1,0,3:T(8,128)(2,1)S(1)} %bitcast.38, bf16[2,32,128,128]{3,1,2,0:T(8,128)(2,1)S(1)} %convolution_convert_fusion), kind=kOutput, calls=%fused_computation | convolution fusion | flops 536870912 | bytes 6422528 | tf_op jit(solution)/shard_map/tcji,tif->cjf/dot_general | solution.py:43
  16.7 50.4 %all-gather.2.cloned.1.call-done = bf16[32,128,256]{2,1,0:T(8,128)(2,1)} async-done(((bf16[2,128,256]{2,1,0:T(8,128)(2,1)}), bf16[32,128,256]{2,1,0:T(8,128)(2,1)}) %all-gather.2.cloned.1.call-update) | async-done | bytes 2097168 | tf_op jit(solution)/shard_map/all_gather | solution.py:24
  67.1 3.9 %fusion.9 = bf16[2,128,256]{2,1,0:T(8,128)(2,1)S(1)} fusion(bf16[2,32,128,128]{3,1,2,0:T(8,128)(2,1)} %copy-done.1, bf16[32,128,256,1]{2,1,0,3:T(8,128)(2,1)} %bitcast.44), kind=kOutput, calls=%fused_computation.12 | convolution fusion | flops 536936448 | bytes 4325376 | tf_op jit(solution)/shard_map/tcji,cjf->tif/dot_general | solution.py:25
  71.4 2.2 %collective-permute-start = (f32[32768]{0:T(1024)S(1)}, f32[32768]{0:T(1024)S(1)}, u32[]{:S(2)}, u32[]{:S(2)}) collective-permute-start(f32[32768]{0:T(1024)S(1)} %bitcast.43), channel_id=1, source_target_pairs={{0,64},{1,65},{2,66},{3,67},{4,68},{5,69},{6,70},{7,71},{8,72},{9,... | collective-permute-start | bytes 393224 | tf_op jit(solution)/shard_map/ppermute | solution.py:71
  74.7 1.9 %collective-permute-start.1 = (f32[16384]{0:T(1024)S(1)}, f32[16384]{0:T(1024)S(1)}, u32[]{:S(2)}, u32[]{:S(2)}) collective-permute-start(f32[16384]{0:T(1024)S(1)} %slice_select_fusion), channel_id=1, source_target_pairs={{0,1},{1,0},{2,3},{3,2},{4,5},{5,4},{6,7},{7,6},{8,9},{9,8},{10,11... | collective-permute-start | bytes 196616 | tf_op jit(solution)/shard_map/ppermute | solution.py:71
  76.6 3.1 %collective-permute-done.1 = f32[16384]{0:T(1024)S(1)} collective-permute-done((f32[16384]{0:T(1024)S(1)}, f32[16384]{0:T(1024)S(1)}, u32[]{:S(2)}, u32[]{:S(2)}) %collective-permute-start.1) | collective-permute-done | bytes 65568 | tf_op jit(solution)/shard_map/ppermute | solution.py:71
  79.7 2.3 %collective-permute-start.2 = (f32[16384]{0:T(1024)S(1)}, f32[16384]{0:T(1024)S(1)}, u32[]{:S(2)}, u32[]{:S(2)}) collective-permute-start(f32[16384]{0:T(1024)S(1)} %select_add_fusion), channel_id=1, source_target_pairs={{0,8},{1,9},{2,10},{3,11},{4,12},{5,13},{6,14},{7,15},{8,0},{9,1},... | collective-permute-start | bytes 196616 | tf_op jit(solution)/shard_map/ppermute | solution.py:73
  82.0 2.8 %collective-permute-done.2 = f32[16384]{0:T(1024)S(1)} collective-permute-done((f32[16384]{0:T(1024)S(1)}, f32[16384]{0:T(1024)S(1)}, u32[]{:S(2)}, u32[]{:S(2)}) %collective-permute-start.2) | collective-permute-done | bytes 65568 | tf_op jit(solution)/shard_map/ppermute | solution.py:73
  84.8 1.9 %collective-permute-start.3 = (f32[16384]{0:T(1024)S(1)}, f32[16384]{0:T(1024)S(1)}, u32[]{:S(2)}, u32[]{:S(2)}) collective-permute-start(f32[16384]{0:T(1024)S(1)} %add.50), channel_id=1, source_target_pairs={{0,128},{1,129},{2,130},{3,131},{4,132},{5,133},{6,134},{7,135},{8... | collective-permute-start | bytes 196616 | tf_op jit(solution)/shard_map/ppermute | solution.py:73
  86.8 3.2 %collective-permute-done.3 = f32[16384]{0:T(1024)S(1)} collective-permute-done((f32[16384]{0:T(1024)S(1)}, f32[16384]{0:T(1024)S(1)}, u32[]{:S(2)}, u32[]{:S(2)}) %collective-permute-start.3) | collective-permute-done | bytes 65568 | tf_op jit(solution)/shard_map/ppermute | solution.py:73
  90.0 3.8 %collective-permute-start.4 = (f32[16384]{0:T(1024)S(1)}, f32[16384]{0:T(1024)S(1)}, u32[]{:S(2)}, u32[]{:S(2)}) collective-permute-start(f32[16384]{0:T(1024)S(1)} %add.51), channel_id=1, source_target_pairs={{0,2},{1,3},{2,0},{3,1},{4,6},{5,7},{6,4},{7,5},{8,10},{9,11},{10,... | collective-permute-start | bytes 196616 | tf_op jit(solution)/shard_map/ppermute | solution.py:73
  93.7 2.1 %collective-permute-done.4 = f32[16384]{0:T(1024)S(1)} collective-permute-done((f32[16384]{0:T(1024)S(1)}, f32[16384]{0:T(1024)S(1)}, u32[]{:S(2)}, u32[]{:S(2)}) %collective-permute-start.4) | collective-permute-done | bytes 65568 | tf_op jit(solution)/shard_map/ppermute | solution.py:73
  95.9 7.6 %collective-permute-start.5 = (f32[16384]{0:T(1024)S(1)}, f32[16384]{0:T(1024)S(1)}, u32[]{:S(2)}, u32[]{:S(2)}) collective-permute-start(f32[16384]{0:T(1024)S(1)} %add.52), channel_id=1, source_target_pairs={{0,4},{1,5},{2,6},{3,7},{4,0},{5,1},{6,2},{7,3},{8,12},{9,13},{10,... | collective-permute-start | bytes 196616 | tf_op jit(solution)/shard_map/ppermute | solution.py:73
  103.5 1.7 %collective-permute-done.5 = f32[16384]{0:T(1024)S(1)} collective-permute-done((f32[16384]{0:T(1024)S(1)}, f32[16384]{0:T(1024)S(1)}, u32[]{:S(2)}, u32[]{:S(2)}) %collective-permute-start.5) | collective-permute-done | bytes 65568 | tf_op jit(solution)/shard_map/ppermute | solution.py:73
  105.2 4.7 %collective-permute-start.6 = (f32[16384]{0:T(1024)S(1)}, f32[16384]{0:T(1024)S(1)}, u32[]{:S(2)}, u32[]{:S(2)}) collective-permute-start(f32[16384]{0:T(1024)S(1)} %add.53), channel_id=1, source_target_pairs={{0,16},{1,17},{2,18},{3,19},{4,20},{5,21},{6,22},{7,23},{8,24},{9,... | collective-permute-start | bytes 196616 | tf_op jit(solution)/shard_map/ppermute | solution.py:73
  111.6 8.7 %collective-permute-start.7 = (f32[16384]{0:T(1024)S(1)}, f32[16384]{0:T(1024)S(1)}, u32[]{:S(2)}, u32[]{:S(2)}) collective-permute-start(f32[16384]{0:T(1024)S(1)} %add.54), channel_id=1, source_target_pairs={{0,32},{1,33},{2,34},{3,35},{4,36},{5,37},{6,38},{7,39},{8,40},{9,... | collective-permute-start | bytes 196616 | tf_op jit(solution)/shard_map/ppermute | solution.py:73
  120.3 2.3 %collective-permute-done.7 = f32[16384]{0:T(1024)S(1)} collective-permute-done((f32[16384]{0:T(1024)S(1)}, f32[16384]{0:T(1024)S(1)}, u32[]{:S(2)}, u32[]{:S(2)}) %collective-permute-start.7) | collective-permute-done | bytes 65568 | tf_op jit(solution)/shard_map/ppermute | solution.py:73
  122.7 2.9 %collective-permute-start.8 = (f32[16384]{0:T(1024)S(1)}, f32[16384]{0:T(1024)S(1)}, u32[]{:S(2)}, u32[]{:S(2)}) collective-permute-start(f32[16384]{0:T(1024)S(1)} %add.55), channel_id=1, source_target_pairs={{0,256},{1,257},{2,258},{3,259},{4,260},{5,261},{6,262},{7,263},{8... | collective-permute-start | bytes 196616 | tf_op jit(solution)/shard_map/ppermute | solution.py:73
  125.6 4.1 %collective-permute-done.8 = f32[16384]{0:T(1024)S(1)} collective-permute-done((f32[16384]{0:T(1024)S(1)}, f32[16384]{0:T(1024)S(1)}, u32[]{:S(2)}, u32[]{:S(2)}) %collective-permute-start.8) | collective-permute-done | bytes 65568 | tf_op jit(solution)/shard_map/ppermute | solution.py:73
  129.7 4.3 %collective-permute-start.9 = (f32[16384]{0:T(1024)S(1)}, f32[16384]{0:T(1024)S(1)}, u32[]{:S(2)}, u32[]{:S(2)}) collective-permute-start(f32[16384]{0:T(1024)S(1)} %add.56), channel_id=1, source_target_pairs={{0,512},{1,513},{2,514},{3,515},{4,516},{5,517},{6,518},{7,519},{8... | collective-permute-start | bytes 196616 | tf_op jit(solution)/shard_map/ppermute | solution.py:73
  134.1 5.2 %collective-permute-done.9 = f32[16384]{0:T(1024)S(1)} collective-permute-done((f32[16384]{0:T(1024)S(1)}, f32[16384]{0:T(1024)S(1)}, u32[]{:S(2)}, u32[]{:S(2)}) %collective-permute-start.9) | collective-permute-done | bytes 65568 | tf_op jit(solution)/shard_map/ppermute | solution.py:73
  139.2 2.3 %collective-permute-start.10 = (f32[16384]{0:T(1024)S(1)}, f32[16384]{0:T(1024)S(1)}, u32[]{:S(2)}, u32[]{:S(2)}) collective-permute-start(f32[16384]{0:T(1024)S(1)} %add.57), channel_id=1, source_target_pairs={{0,1},{1,0},{2,3},{3,2},{4,5},{5,4},{6,7},{7,6},{8,9},{9,8},{10,11... | collective-permute-start | bytes 196616 | tf_op jit(solution)/shard_map/ppermute | solution.py:76
  141.5 2.7 %collective-permute-done.10 = f32[16384]{0:T(1024)S(1)} collective-permute-done((f32[16384]{0:T(1024)S(1)}, f32[16384]{0:T(1024)S(1)}, u32[]{:S(2)}, u32[]{:S(2)}) %collective-permute-start.10) | collective-permute-done | bytes 65568 | tf_op jit(solution)/shard_map/ppermute | solution.py:76
  144.3 12.4 %collective-permute-start.11 = (f32[32768]{0:T(1024)S(1)}, f32[32768]{0:T(1024)S(1)}, u32[]{:S(2)}, u32[]{:S(2)}) collective-permute-start(f32[32768]{0:T(1024)S(1)} %pad_maximum_fusion.1), channel_id=1, source_target_pairs={{0,64},{1,65},{2,66},{3,67},{4,68},{5,69},{6,70},{7,71},{8,72},{9,... | collective-permute-start | bytes 393224 | tf_op jit(solution)/shard_map/ppermute | solution.py:76
  (45 shorter events, 12.7 us)
Async XLA Ops:
  7.2 3.4 %copy-start = (bf16[2,24,128,128]{3,2,1,0:T(8,128)(2,1)S(1)}, bf16[2,24,128,128]{3,2,1,0:T(8,128)(2,1)}, u32[]{:S(2)}) copy-start(bf16[2,24,128,128]{3,2,1,0:T(8,128)(2,1)} %param.9) | copy-start | bytes 4718596
  7.2 59.9 %all-gather.2.cloned.1.call-start = ((), (), s32[]{:S(2)}) async-start(), calls=%async_computation.1 | async-start | bytes 2228224 | tf_op jit(solution)/shard_map/all_gather | solution.py:24
  7.9 150.5 %reduce-scatter.2.cloned.1.call-start = ((), (), s32[]{:S(2)}) async-start(), calls=%async_computation.2 | async-start | bytes 4456448 | tf_op jit(solution)/shard_map/reduce_scatter | solution.py:42
  12.0 1.4 copy-start.1
  67.1 3.9 %copy-start.3 = (bf16[2,128,256]{2,1,0:T(8,128)(2,1)S(1)}, bf16[2,128,256]{2,1,0:T(8,128)(2,1)}, u32[]{:S(2)}) copy-start(bf16[2,128,256]{2,1,0:T(8,128)(2,1)} %param.12) | copy-start | bytes 393220
  71.3 85.4 %copy-start.2 = (bf16[256,256]{1,0:T(8,128)(2,1)S(1)}, bf16[256,256]{1,0:T(8,128)(2,1)}, u32[]{:S(2)}) copy-start(bf16[256,256]{1,0:T(8,128)(2,1)} %param.8) | copy-start | bytes 393220
  71.4 3.2 %collective-permute-start = (f32[32768]{0:T(1024)S(1)}, f32[32768]{0:T(1024)S(1)}, u32[]{:S(2)}, u32[]{:S(2)}) collective-permute-start(f32[32768]{0:T(1024)S(1)} %bitcast.43), channel_id=1, source_target_pairs={{0,64},{1,65},{2,66},{3,67},{4,68},{5,69},{6,70},{7,71},{8,72},{9,... | collective-permute-start | bytes 393224 | tf_op jit(solution)/shard_map/ppermute | solution.py:71
  74.7 5.0 %collective-permute-start.1 = (f32[16384]{0:T(1024)S(1)}, f32[16384]{0:T(1024)S(1)}, u32[]{:S(2)}, u32[]{:S(2)}) collective-permute-start(f32[16384]{0:T(1024)S(1)} %slice_select_fusion), channel_id=1, source_target_pairs={{0,1},{1,0},{2,3},{3,2},{4,5},{5,4},{6,7},{7,6},{8,9},{9,8},{10,11... | collective-permute-start | bytes 196616 | tf_op jit(solution)/shard_map/ppermute | solution.py:71
  79.7 78.8 %copy-start.4 = (s32[2,128,256]{2,1,0:T(8,128)S(1)}, s32[2,128,256]{2,1,0:T(8,128)}, u32[]{:S(2)}) copy-start(s32[2,128,256]{2,1,0:T(8,128)} %param.13) | copy-start | bytes 786436
  79.7 5.1 %collective-permute-start.2 = (f32[16384]{0:T(1024)S(1)}, f32[16384]{0:T(1024)S(1)}, u32[]{:S(2)}, u32[]{:S(2)}) collective-permute-start(f32[16384]{0:T(1024)S(1)} %select_add_fusion), channel_id=1, source_target_pairs={{0,8},{1,9},{2,10},{3,11},{4,12},{5,13},{6,14},{7,15},{8,0},{9,1},... | collective-permute-start | bytes 196616 | tf_op jit(solution)/shard_map/ppermute | solution.py:73
  84.8 5.1 %collective-permute-start.3 = (f32[16384]{0:T(1024)S(1)}, f32[16384]{0:T(1024)S(1)}, u32[]{:S(2)}, u32[]{:S(2)}) collective-permute-start(f32[16384]{0:T(1024)S(1)} %add.50), channel_id=1, source_target_pairs={{0,128},{1,129},{2,130},{3,131},{4,132},{5,133},{6,134},{7,135},{8... | collective-permute-start | bytes 196616 | tf_op jit(solution)/shard_map/ppermute | solution.py:73
  90.0 5.9 %collective-permute-start.4 = (f32[16384]{0:T(1024)S(1)}, f32[16384]{0:T(1024)S(1)}, u32[]{:S(2)}, u32[]{:S(2)}) collective-permute-start(f32[16384]{0:T(1024)S(1)} %add.51), channel_id=1, source_target_pairs={{0,2},{1,3},{2,0},{3,1},{4,6},{5,7},{6,4},{7,5},{8,10},{9,11},{10,... | collective-permute-start | bytes 196616 | tf_op jit(solution)/shard_map/ppermute | solution.py:73
  95.9 9.3 %collective-permute-start.5 = (f32[16384]{0:T(1024)S(1)}, f32[16384]{0:T(1024)S(1)}, u32[]{:S(2)}, u32[]{:S(2)}) collective-permute-start(f32[16384]{0:T(1024)S(1)} %add.52), channel_id=1, source_target_pairs={{0,4},{1,5},{2,6},{3,7},{4,0},{5,1},{6,2},{7,3},{8,12},{9,13},{10,... | collective-permute-start | bytes 196616 | tf_op jit(solution)/shard_map/ppermute | solution.py:73
  105.2 6.4 %collective-permute-start.6 = (f32[16384]{0:T(1024)S(1)}, f32[16384]{0:T(1024)S(1)}, u32[]{:S(2)}, u32[]{:S(2)}) collective-permute-start(f32[16384]{0:T(1024)S(1)} %add.53), channel_id=1, source_target_pairs={{0,16},{1,17},{2,18},{3,19},{4,20},{5,21},{6,22},{7,23},{8,24},{9,... | collective-permute-start | bytes 196616 | tf_op jit(solution)/shard_map/ppermute | solution.py:73
  111.6 11.1 %collective-permute-start.7 = (f32[16384]{0:T(1024)S(1)}, f32[16384]{0:T(1024)S(1)}, u32[]{:S(2)}, u32[]{:S(2)}) collective-permute-start(f32[16384]{0:T(1024)S(1)} %add.54), channel_id=1, source_target_pairs={{0,32},{1,33},{2,34},{3,35},{4,36},{5,37},{6,38},{7,39},{8,40},{9,... | collective-permute-start | bytes 196616 | tf_op jit(solution)/shard_map/ppermute | solution.py:73
  122.7 7.0 %collective-permute-start.8 = (f32[16384]{0:T(1024)S(1)}, f32[16384]{0:T(1024)S(1)}, u32[]{:S(2)}, u32[]{:S(2)}) collective-permute-start(f32[16384]{0:T(1024)S(1)} %add.55), channel_id=1, source_target_pairs={{0,256},{1,257},{2,258},{3,259},{4,260},{5,261},{6,262},{7,263},{8... | collective-permute-start | bytes 196616 | tf_op jit(solution)/shard_map/ppermute | solution.py:73
  129.7 9.5 %collective-permute-start.9 = (f32[16384]{0:T(1024)S(1)}, f32[16384]{0:T(1024)S(1)}, u32[]{:S(2)}, u32[]{:S(2)}) collective-permute-start(f32[16384]{0:T(1024)S(1)} %add.56), channel_id=1, source_target_pairs={{0,512},{1,513},{2,514},{3,515},{4,516},{5,517},{6,518},{7,519},{8... | collective-permute-start | bytes 196616 | tf_op jit(solution)/shard_map/ppermute | solution.py:73
  139.2 5.0 %collective-permute-start.10 = (f32[16384]{0:T(1024)S(1)}, f32[16384]{0:T(1024)S(1)}, u32[]{:S(2)}, u32[]{:S(2)}) collective-permute-start(f32[16384]{0:T(1024)S(1)} %add.57), channel_id=1, source_target_pairs={{0,1},{1,0},{2,3},{3,2},{4,5},{5,4},{6,7},{7,6},{8,9},{9,8},{10,11... | collective-permute-start | bytes 196616 | tf_op jit(solution)/shard_map/ppermute | solution.py:76
  144.3 13.3 %collective-permute-start.11 = (f32[32768]{0:T(1024)S(1)}, f32[32768]{0:T(1024)S(1)}, u32[]{:S(2)}, u32[]{:S(2)}) collective-permute-start(f32[32768]{0:T(1024)S(1)} %pad_maximum_fusion.1), channel_id=1, source_target_pairs={{0,64},{1,65},{2,66},{3,67},{4,68},{5,69},{6,70},{7,71},{8,72},{9,... | collective-permute-start | bytes 393224 | tf_op jit(solution)/shard_map/ppermute | solution.py:76
Sparse Core Ops, SparseCore 0:
  10.7 56.3 all-gather.1
  70.5 67.9 reduce-scatter.1
